TPU v7x, 128 devices: a whole 4x4x4 slice. The times are simulated.
128 devices in a mesh: seq: 32 (over y, z, core), tp: 4 (over x).
Axes of the slice: x: 4, y: 4, z: 4, core: 2. Of those that a mesh axis runs over, the one named last changes fastest.
Arguments:
- query_rows: bfloat16 [16384, 2560], P(('seq', 'tp')), may hold values from -6 to 6
- key_rows: bfloat16 [16384, 512], P(('seq', 'tp')), may hold values from -6 to 6
- value_rows: bfloat16 [16384, 512], P(('seq', 'tp')), may hold values from -6 to 6
- out_grad: bfloat16 [16384, 2560], P(('seq', 'tp')), may hold values from -6 to 6
- doc_lengths: int32 [8], replicated, may hold values from 1 to 4096, as said below
Outputs:
- attended: bfloat16 [16384, 2560], P(('seq', 'tp'))
- query_grad: bfloat16 [16384, 2560], P(('seq', 'tp'))
- key_grad: bfloat16 [16384, 512], P(('seq', 'tp'))
- value_grad: bfloat16 [16384, 512], P(('seq', 'tp'))
Inputs may be any that keep to these rules, and one draw needn't show every extreme that they name: `doc_lengths`: 8 document lengths in token order that sum to 16384; exactly one of them is 4096, all others are shorter.
All inputs are finite; a program needn't handle non-finite values.
Results may differ from a plain program's by a relative error of at most 0.022.
Values may be sent and summed in bfloat16 or wider, within the bound.
No kernel may reach another device: no remote copies, remote signals or barrier semaphores. Data moves between devices by JAX's collectives and lax.ppermute only.
A program may use at most 64 MiB of HBM per device.

v0:
```python
import math

import jax
import jax.numpy as jnp
from jax import lax
from jax.sharding import PartitionSpec as P

HD = 128
QH = 20
KVH = 4


def passed_along(value, axis, by):
    peers = lax.axis_size(axis)
    pairs = [(i, i + by) for i in range(peers) if 0 <= i + by < peers]
    return lax.ppermute(value, axis, pairs)


def passed_along_2(block, axis, distance):
    devices = range(lax.axis_size(axis))
    route = [((i - distance) % len(devices), i) for i in devices]
    return lax.ppermute(block, axis, route)


def placed(first_row, row_count, doc_ends):
    position = first_row + jnp.arange(row_count, dtype=jnp.int32)
    segment = jnp.sum((position[:, None] >= doc_ends[None, :]).astype(jnp.int32), axis=1)
    return (position, segment)


def allowed(query_pos, query_seg, key_pos, key_seg):
    return (
        (key_pos[None, :] <= query_pos[:, None])
        & (key_pos[None, :] >= 0)
        & (key_seg[None, :] == query_seg[:, None])
    )


def absorb(softmax_state, query_heads, key_block, value_block, visible, scaling):
    running, denominator, accumulated = softmax_state
    scores = (
        jnp.einsum("bkgd,tkd->bkgt", query_heads, key_block, preferred_element_type=jnp.float32)
        * scaling
    )
    spread = visible[:, None, None, :]
    scores = jnp.where(spread, scores, -1e30)
    newest = jnp.maximum(running, jnp.max(scores, axis=-1))
    weight = jnp.where(spread, jnp.exp(scores - newest[..., None]), 0.0)
    shrink = jnp.exp(running - newest)
    denominator = denominator * shrink + jnp.sum(weight, axis=-1)
    accumulated = accumulated * shrink[..., None] + jnp.einsum(
        "bkgt,tkd->bkgd",
        weight.astype(jnp.bfloat16),
        value_block,
        preferred_element_type=jnp.float32,
    )
    return (newest, denominator, accumulated)


def contrib(query_heads, grad_heads, log_total, row_dot, key_block, value_block, visible, scaling):
    scores = (
        jnp.einsum("bkgd,tkd->bkgt", query_heads, key_block, preferred_element_type=jnp.float32)
        * scaling
    )
    spread = visible[:, None, None, :]
    scores = jnp.where(spread, scores, -1e30)
    probability = jnp.where(spread, jnp.exp(scores - log_total[..., None]), 0.0)
    value_part = jnp.einsum(
        "bkgt,bkgd->tkd",
        probability.astype(jnp.bfloat16),
        grad_heads,
        preferred_element_type=jnp.float32,
    )
    grad_prob = jnp.einsum(
        "bkgd,tkd->bkgt", grad_heads, value_block, preferred_element_type=jnp.float32
    )
    grad_score = (probability * (grad_prob - row_dot[..., None])).astype(jnp.bfloat16)
    query_part = (
        jnp.einsum("bkgt,tkd->bkgd", grad_score, key_block, preferred_element_type=jnp.float32)
        * scaling
    )
    key_part = (
        jnp.einsum("bkgt,bkgd->tkd", grad_score, query_heads, preferred_element_type=jnp.float32)
        * scaling
    )
    return (query_part, key_part, value_part)


def per_device(query_rows, key_rows, value_rows, out_grad, doc_lengths):
    per_kv = QH // KVH
    scaling = HD ** (-0.5)
    query_here, key_here, value_here, grad_here = (
        lax.all_to_all(query_rows, "tp", split_axis=1, concat_axis=0, tiled=True),
        lax.all_to_all(key_rows, "tp", split_axis=1, concat_axis=0, tiled=True),
        lax.all_to_all(value_rows, "tp", split_axis=1, concat_axis=0, tiled=True),
        lax.all_to_all(out_grad, "tp", split_axis=1, concat_axis=0, tiled=True),
    )
    length = query_here.shape[0]
    kv_heads = key_here.shape[1] // HD
    query_heads = query_here.reshape(length, kv_heads, per_kv, HD)
    grad_heads = grad_here.reshape(length, kv_heads, per_kv, HD)
    seq_count = lax.axis_size("seq")
    position = lax.axis_index("seq")
    doc_ends = jnp.cumsum(doc_lengths)
    query_pos, query_seg = placed(position * length, length, doc_ends)
    span_rows = math.gcd(length, 512)

    def sweep_keys(softmax_state, key_piece, value_piece, first_row):

        def sweep_advance(block_index, current):
            offset = block_index * span_rows
            key_block = key_piece.reshape(span_rows, kv_heads, HD)
            value_block = value_piece.reshape(span_rows, kv_heads, HD)
            key_pos, key_seg = placed(first_row + offset, span_rows, doc_ends)
            visible = allowed(query_pos, query_seg, key_pos, key_seg)
            return lax.cond(
                jnp.any(visible),
                lambda carried: absorb(
                    carried, query_heads, key_block, value_block, visible, scaling
                ),
                lambda carried: carried,
                current,
            )

        return lax.fori_loop(0, length // span_rows, sweep_advance, softmax_state)

    initial = (
        jnp.full((length, kv_heads, per_kv), -1e30, jnp.float32),
        jnp.zeros((length, kv_heads, per_kv), jnp.float32),
        jnp.zeros((length, kv_heads, per_kv, HD), jnp.float32),
    )
    softmax_state = sweep_keys(initial, key_here, value_here, position * length)

    def travel(turn_index, carried):
        current, key_value = carried
        key_value = passed_along(key_value, "seq", 1)
        current = sweep_keys(current, key_value[0], key_value[1], (position - turn_index) * length)
        return (current, key_value)

    softmax_state, spent = lax.fori_loop(
        1, seq_count, travel, (softmax_state, jnp.stack((key_here, value_here)))
    )
    running, denominator, accumulated = softmax_state
    out_heads = (accumulated / denominator[..., None]).astype(jnp.bfloat16)
    log_total = running + jnp.log(denominator)
    row_dot = jnp.sum(grad_heads.astype(jnp.float32) * out_heads.astype(jnp.float32), axis=-1)

    def backward_turn(turn_index, carried):
        query_acc, key_value, grad_sums = carried
        source_shard = (position - turn_index) % seq_count

        def backward_advance(block_index, inner_carry):
            query_inner, sums_inner = inner_carry
            offset = block_index * span_rows
            key_block = key_value[0].reshape(span_rows, kv_heads, HD)
            value_block = key_value[1].reshape(span_rows, kv_heads, HD)
            key_pos, key_seg = placed(source_shard * length + offset, span_rows, doc_ends)
            visible = allowed(query_pos, query_seg, key_pos, key_seg)

            def compute(unused):
                query_part, key_part, value_part = contrib(
                    query_heads,
                    grad_heads,
                    log_total,
                    row_dot,
                    key_block,
                    value_block,
                    visible,
                    scaling,
                )
                return (
                    query_part,
                    jnp.stack((key_part.reshape(span_rows, -1), value_part.reshape(span_rows, -1))),
                )

            def nothing(unused):
                return (
                    jnp.zeros_like(query_inner),
                    jnp.zeros((2, span_rows, key_value.shape[2]), jnp.float32),
                )

            query_part, key_value_part = lax.cond(jnp.any(visible), compute, nothing, 0)
            current = sums_inner
            sums_inner = current + key_value_part
            return (query_inner + query_part, sums_inner)

        query_acc, grad_sums = lax.fori_loop(
            0, length // span_rows, backward_advance, (query_acc, grad_sums)
        )
        key_value = passed_along(key_value, "seq", 1)
        grad_sums = passed_along_2(grad_sums.astype(jnp.bfloat16), "seq", 1).astype(grad_sums.dtype)
        return (query_acc, key_value, grad_sums)

    key_value = jnp.stack((key_here, value_here))
    start_sums = jnp.zeros(key_value.shape, jnp.float32)
    start_query = jnp.zeros((length, kv_heads, per_kv, HD), jnp.float32)
    query_acc, spent_pair, grad_sums = lax.fori_loop(
        0, seq_count, backward_turn, (start_query, key_value, start_sums)
    )
    outputs = (
        lax.all_to_all(
            out_heads.reshape(length, -1), "tp", split_axis=0, concat_axis=1, tiled=True
        ),
        lax.all_to_all(
            query_acc.astype(jnp.bfloat16).reshape(length, -1),
            "tp",
            split_axis=0,
            concat_axis=1,
            tiled=True,
        ),
        lax.all_to_all(
            grad_sums[0].astype(jnp.bfloat16), "tp", split_axis=0, concat_axis=1, tiled=True
        ),
        lax.all_to_all(
            grad_sums[1].astype(jnp.bfloat16), "tp", split_axis=0, concat_axis=1, tiled=True
        ),
    )
    return (outputs[0], outputs[1], outputs[2], outputs[3])


def solution(mesh):
    return jax.shard_map(
        per_device,
        mesh=mesh,
        in_specs=(
            P(("seq", "tp"), None),
            P(("seq", "tp"), None),
            P(("seq", "tp"), None),
            P(("seq", "tp"), None),
            P(),
        ),
        out_specs=(
            P(("seq", "tp"), None),
            P(("seq", "tp"), None),
            P(("seq", "tp"), None),
            P(("seq", "tp"), None),
        ),
        check_vma=False,
    )
```

profile of v0, /device:TPU:16, one launch (start us, length us, event | category | flops | bytes accessed | tf_op | source)
XLA Modules:
  0.0 950.4 jit_solution(5887042369976095308)
XLA Ops:
  15.9 5.9 all-to-all-done.2
  40.6 10.6 %conditional.3 = ((f32[512,1,5]{0,2,1:T(8,128)S(1)}, f32[512,1,5]{0,2,1:T(8,128)S(1)}, f32[512,1,5,128]{3,0,2,1:T(8,128)})) conditional(s32[]{:T(128)} %convert_element_type.110, (f32[512,1,5]{0,2,1:T(8,128)S(1)}, f32[512,1,5]{0,2,1:T(8,128)S(1)}, f32[512,1,5,128]{3,0,2,1:T(8,128)}) %tuple.76, (pred[512,512]{0,1:T(8,128)(4,1)S(1)}, ...), branch_computations={%region_3.4_spmd, %region_4.7_spmd} | conditional | flops 688791040 | bytes 41713724 | solution.py:116
  45.5 5.7 fusion.14
  51.2 331.4 %while.74 = (s32[]{:T(128)}, f32[512,1,5]{0,2,1:T(8,128)S(1)}, f32[512,1,5]{0,2,1:T(8,128)S(1)}, f32[512,1,5,128]{3,0,2,1:T(8,128)}, bf16[2,512,128]{2,1,0:T(8,1...) while((s32[]{:T(128)}, f32[512,1,5]{0,2,1:T(8,128)S(1)}, ...), condition=%wide.region_14.15_spmd.clone, body=%wide.region_7.14_spmd.clone.sunk | while | flops 690115584 | bytes 22082896 | solution.py:140
  56.2 4.8 collective-permute-done
  61.0 6.2 conditional.8
  96.8 5.5 collective-permute-start
  113.2 6.9 collective-permute-done
  125.1 8.9 collective-permute-done
  139.1 8.9 collective-permute-done
  153.1 8.9 collective-permute-done
  167.0 8.9 collective-permute-done
  391.7 509.3 %while.75 = (s32[]{:T(128)}, f32[512,1,5,128]{3,0,2,1:T(8,128)}, bf16[2,512,128]{2,1,0:T(8,128)(2,1)S(1)}, f32[2,512,128]{2,1,0:T(8,128)S(1)}, s32[]{:T(128)}, /...) while((s32[]{:T(128)}, f32[512,1,5,128]{3,0,2,1:T(8,128)}, ...), condition=%wide.region_21.22_spmd.clone, body=%wide.region_16.21_spmd.clone.sunk | while | flops 1696478720 | bytes 41610760 | solution.py:197
  397.4 9.5 %conditional.9 = (f32[512,1,5,128]{3,0,2,1:T(8,128)S(1)}, f32[2,512,128]{2,1,0:T(8,128)S(1)}) conditional(s32[]{:T(128)} %convert_element_type.166, () %tuple.146, (pred[512,512]{0,1:T(8,128)(4,1)S(1)}, bf16[2,512,128]{2,1,0:T(8,128)(2,1)}, bf16[512,1,5,128]{3,0,2,1:T(8,128)(2,1)S(1)}, f32[512,1,5]{0,2,1:T(8,128)}, ...), branch_computations={%region_19.19_spmd, %region_20.20_spmd} | conditional | flops 1693974528 | bytes 32679980 | solution.py:182
  408.4 6.6 collective-permute-done.2
  420.8 9.5 %conditional.9 = (f32[512,1,5,128]{3,0,2,1:T(8,128)S(1)}, f32[2,512,128]{2,1,0:T(8,128)S(1)}) conditional(s32[]{:T(128)} %convert_element_type.166, () %tuple.146, (pred[512,512]{0,1:T(8,128)(4,1)S(1)}, bf16[2,512,128]{2,1,0:T(8,128)(2,1)}, bf16[512,1,5,128]{3,0,2,1:T(8,128)(2,1)S(1)}, f32[512,1,5]{0,2,1:T(8,128)}, ...), branch_computations={%region_19.19_spmd, %region_20.20_spmd} | conditional | flops 1693974528 | bytes 32679980 | solution.py:182
  433.1 5.3 collective-permute-done.2
  467.2 7.6 collective-permute-start.1
  499.4 8.1 collective-permute-done.2
  516.1 12.6 %collective-permute-done.2 = bf16[2,512,128]{2,1,0:T(8,128)(2,1)S(1)} collective-permute-done((bf16[2,512,128]{2,1,0:T(8,128)(2,1)S(1)}, bf16[2,512,128]{2,1,0:T(8,128)(2,1)S(1)}, u32[]{:S(2)}, u32[]{:S(2)}) %collective-permute-start.2) | collective-permute-done | bytes 262176 | tf_op jit(solution)/shard_map/while/body/eval_jaxpr/ppermute | solution.py:22
  537.4 12.6 %collective-permute-done.2 = bf16[2,512,128]{2,1,0:T(8,128)(2,1)S(1)} collective-permute-done((bf16[2,512,128]{2,1,0:T(8,128)(2,1)S(1)}, bf16[2,512,128]{2,1,0:T(8,128)(2,1)S(1)}, u32[]{:S(2)}, u32[]{:S(2)}) %collective-permute-start.2) | collective-permute-done | bytes 262176 | tf_op jit(solution)/shard_map/while/body/eval_jaxpr/ppermute | solution.py:22
  558.7 12.6 %collective-permute-done.2 = bf16[2,512,128]{2,1,0:T(8,128)(2,1)S(1)} collective-permute-done((bf16[2,512,128]{2,1,0:T(8,128)(2,1)S(1)}, bf16[2,512,128]{2,1,0:T(8,128)(2,1)S(1)}, u32[]{:S(2)}, u32[]{:S(2)}) %collective-permute-start.2) | collective-permute-done | bytes 262176 | tf_op jit(solution)/shard_map/while/body/eval_jaxpr/ppermute | solution.py:22
  580.0 12.6 %collective-permute-done.2 = bf16[2,512,128]{2,1,0:T(8,128)(2,1)S(1)} collective-permute-done((bf16[2,512,128]{2,1,0:T(8,128)(2,1)S(1)}, bf16[2,512,128]{2,1,0:T(8,128)(2,1)S(1)}, u32[]{:S(2)}, u32[]{:S(2)}) %collective-permute-start.2) | collective-permute-done | bytes 262176 | tf_op jit(solution)/shard_map/while/body/eval_jaxpr/ppermute | solution.py:22
  601.3 5.3 collective-permute-done.2
  615.3 5.3 collective-permute-done.2
  629.3 5.3 collective-permute-done.2
  643.3 5.3 collective-permute-done.2
  657.3 5.3 collective-permute-done.2
  671.4 5.3 collective-permute-done.2
  685.4 5.3 collective-permute-done.2
  699.4 5.3 collective-permute-done.2
  713.4 5.3 collective-permute-done.2
  727.4 5.3 collective-permute-done.2
  741.5 5.3 collective-permute-done.2
  755.5 5.3 collective-permute-done.2
  769.5 5.3 collective-permute-done.2
  783.5 5.3 collective-permute-done.2
  797.5 5.3 collective-permute-done.2
  811.5 5.3 collective-permute-done.2
  825.6 5.3 collective-permute-done.2
  839.6 5.3 collective-permute-done.2
  853.6 5.3 collective-permute-done.2
  867.6 5.3 collective-permute-done.2
  881.6 5.3 collective-permute-done.2
  895.6 5.3 collective-permute-done.2
  901.8 10.8 %all_to_all.134 = bf16[4,128,128]{2,1,0:T(8,128)(2,1)S(1)} all-to-all(bf16[4,128,128]{2,1,0:T(8,128)(2,1)S(1)} %bitcast.260), channel_id=1, replica_groups=mesh['seq'=32,'tp'=4] {'tp'}, dimensions={0} | all-to-all | bytes 262144 | tf_op jit(solution)/shard_map/all_to_all | solution.py:211
  927.1 10.0 %all-to-all-done.5 = bf16[4,128,640]{1,2,0:T(8,128)(2,1)S(1)} async-done(((bf16[4,128,640]{1,2,0:T(8,128)(2,1)}), bf16[4,128,640]{1,2,0:T(8,128)(2,1)S(1)}, u32[]{:S(2)}, u32[]{:S(2)}) %all-to-all-start.5) | async-done | bytes 655392 | tf_op jit(solution)/shard_map/all_to_all | solution.py:204
  943.4 5.8 all-to-all-done.3
  (834 shorter events, 620.6 us)
Async XLA Ops:
  2.3 10.3 %all-to-all-start = ((bf16[128,4,128]{0,2,1:T(8,128)(2,1)}), bf16[128,4,128]{0,2,1:T(8,128)(2,1)S(1)}, u32[]{:S(2)}, u32[]{:S(2)}) async-start(bf16[128,4,128]{0,2,1:T(8,128)(2,1)} %bitcast.59), calls=%async_computation | async-start | bytes 262144 | tf_op jit(solution)/shard_map/all_to_all | solution.py:94
  21.8 12.9 %all-to-all-start.1 = ((bf16[128,4,640]{0,2,1:T(8,128)(2,1)}), bf16[128,4,640]{0,2,1:T(8,128)(2,1)S(1)}, u32[]{:S(2)}, u32[]{:S(2)}) async-start(bf16[128,4,640]{0,2,1:T(8,128)(2,1)} %bitcast.61), calls=%async_computation.1 | async-start | bytes 1310720 | tf_op jit(solution)/shard_map/all_to_all | solution.py:93
  34.8 349.5 %all-to-all-start.4 = ((bf16[128,4,640]{0,2,1:T(8,128)(2,1)}), bf16[128,4,640]{0,2,1:T(8,128)(2,1)}, u32[]{:S(2)}, u32[]{:S(2)}) async-start(bf16[128,4,640]{0,2,1:T(8,128)(2,1)} %bitcast.70), calls=%async_computation.4 | async-start | bytes 1310720 | tf_op jit(solution)/shard_map/all_to_all | solution.py:96
  106.7 13.4 %collective-permute-start = (bf16[2,512,128]{2,1,0:T(8,128)(2,1)S(1)}, bf16[2,512,128]{2,1,0:T(8,128)(2,1)S(1)}, u32[]{:S(2)}, u32[]{:S(2)}) collective-permute-start(bf16[2,512,128]{2,1,0:T(8,128)(2,1)S(1)} %get-tuple-element.1204), channel_id=1, source_target_pairs={{0,4},{4,8},{8,12},{12,16},{16,20},{20,24},{24,28},{28,32},{32,36}... | collective-permute-start | bytes 786440 | tf_op jit(solution)/shard_map/while/body/eval_jaxpr/ppermute | solution.py:16
  120.1 13.9 %collective-permute-start = (bf16[2,512,128]{2,1,0:T(8,128)(2,1)S(1)}, bf16[2,512,128]{2,1,0:T(8,128)(2,1)S(1)}, u32[]{:S(2)}, u32[]{:S(2)}) collective-permute-start(bf16[2,512,128]{2,1,0:T(8,128)(2,1)S(1)} %get-tuple-element.1204), channel_id=1, source_target_pairs={{0,4},{4,8},{8,12},{12,16},{16,20},{20,24},{24,28},{28,32},{32,36}... | collective-permute-start | bytes 786440 | tf_op jit(solution)/shard_map/while/body/eval_jaxpr/ppermute | solution.py:16
  134.1 13.9 %collective-permute-start = (bf16[2,512,128]{2,1,0:T(8,128)(2,1)S(1)}, bf16[2,512,128]{2,1,0:T(8,128)(2,1)S(1)}, u32[]{:S(2)}, u32[]{:S(2)}) collective-permute-start(bf16[2,512,128]{2,1,0:T(8,128)(2,1)S(1)} %get-tuple-element.1204), channel_id=1, source_target_pairs={{0,4},{4,8},{8,12},{12,16},{16,20},{20,24},{24,28},{28,32},{32,36}... | collective-permute-start | bytes 786440 | tf_op jit(solution)/shard_map/while/body/eval_jaxpr/ppermute | solution.py:16
  148.0 13.9 %collective-permute-start = (bf16[2,512,128]{2,1,0:T(8,128)(2,1)S(1)}, bf16[2,512,128]{2,1,0:T(8,128)(2,1)S(1)}, u32[]{:S(2)}, u32[]{:S(2)}) collective-permute-start(bf16[2,512,128]{2,1,0:T(8,128)(2,1)S(1)} %get-tuple-element.1204), channel_id=1, source_target_pairs={{0,4},{4,8},{8,12},{12,16},{16,20},{20,24},{24,28},{28,32},{32,36}... | collective-permute-start | bytes 786440 | tf_op jit(solution)/shard_map/while/body/eval_jaxpr/ppermute | solution.py:16
  162.0 13.9 %collective-permute-start = (bf16[2,512,128]{2,1,0:T(8,128)(2,1)S(1)}, bf16[2,512,128]{2,1,0:T(8,128)(2,1)S(1)}, u32[]{:S(2)}, u32[]{:S(2)}) collective-permute-start(bf16[2,512,128]{2,1,0:T(8,128)(2,1)S(1)} %get-tuple-element.1204), channel_id=1, source_target_pairs={{0,4},{4,8},{8,12},{12,16},{16,20},{20,24},{24,28},{28,32},{32,36}... | collective-permute-start | bytes 786440 | tf_op jit(solution)/shard_map/while/body/eval_jaxpr/ppermute | solution.py:16
  392.4 22.7 %collective-permute-start.1 = (bf16[2,512,128]{2,1,0:T(8,128)(2,1)}, bf16[2,512,128]{2,1,0:T(8,128)(2,1)S(1)}, u32[]{:S(2)}, u32[]{:S(2)}) collective-permute-start(bf16[2,512,128]{2,1,0:T(8,128)(2,1)} %copy.171), channel_id=1, source_target_pairs={{0,4},{4,8},{8,12},{12,16},{16,20},{20,24},{24,28},{28,32},{32,36}... | collective-permute-start | bytes 786440 | tf_op jit(solution)/shard_map/while/body/eval_jaxpr/ppermute | solution.py:16
  415.8 22.7 %collective-permute-start.1 = (bf16[2,512,128]{2,1,0:T(8,128)(2,1)}, bf16[2,512,128]{2,1,0:T(8,128)(2,1)S(1)}, u32[]{:S(2)}, u32[]{:S(2)}) collective-permute-start(bf16[2,512,128]{2,1,0:T(8,128)(2,1)} %copy.171), channel_id=1, source_target_pairs={{0,4},{4,8},{8,12},{12,16},{16,20},{20,24},{24,28},{28,32},{32,36}... | collective-permute-start | bytes 786440 | tf_op jit(solution)/shard_map/while/body/eval_jaxpr/ppermute | solution.py:16
  439.2 13.3 %collective-permute-start.1 = (bf16[2,512,128]{2,1,0:T(8,128)(2,1)}, bf16[2,512,128]{2,1,0:T(8,128)(2,1)S(1)}, u32[]{:S(2)}, u32[]{:S(2)}) collective-permute-start(bf16[2,512,128]{2,1,0:T(8,128)(2,1)} %copy.171), channel_id=1, source_target_pairs={{0,4},{4,8},{8,12},{12,16},{16,20},{20,24},{24,28},{28,32},{32,36}... | collective-permute-start | bytes 786440 | tf_op jit(solution)/shard_map/while/body/eval_jaxpr/ppermute | solution.py:16
  453.2 13.3 %collective-permute-start.1 = (bf16[2,512,128]{2,1,0:T(8,128)(2,1)}, bf16[2,512,128]{2,1,0:T(8,128)(2,1)S(1)}, u32[]{:S(2)}, u32[]{:S(2)}) collective-permute-start(bf16[2,512,128]{2,1,0:T(8,128)(2,1)} %copy.171), channel_id=1, source_target_pairs={{0,4},{4,8},{8,12},{12,16},{16,20},{20,24},{24,28},{28,32},{32,36}... | collective-permute-start | bytes 786440 | tf_op jit(solution)/shard_map/while/body/eval_jaxpr/ppermute | solution.py:16
  467.2 19.0 %collective-permute-start.1 = (bf16[2,512,128]{2,1,0:T(8,128)(2,1)}, bf16[2,512,128]{2,1,0:T(8,128)(2,1)S(1)}, u32[]{:S(2)}, u32[]{:S(2)}) collective-permute-start(bf16[2,512,128]{2,1,0:T(8,128)(2,1)} %copy.171), channel_id=1, source_target_pairs={{0,4},{4,8},{8,12},{12,16},{16,20},{20,24},{24,28},{28,32},{32,36}... | collective-permute-start | bytes 786440 | tf_op jit(solution)/shard_map/while/body/eval_jaxpr/ppermute | solution.py:16
  486.9 20.6 %collective-permute-start.1 = (bf16[2,512,128]{2,1,0:T(8,128)(2,1)}, bf16[2,512,128]{2,1,0:T(8,128)(2,1)S(1)}, u32[]{:S(2)}, u32[]{:S(2)}) collective-permute-start(bf16[2,512,128]{2,1,0:T(8,128)(2,1)} %copy.171), channel_id=1, source_target_pairs={{0,4},{4,8},{8,12},{12,16},{16,20},{20,24},{24,28},{28,32},{32,36}... | collective-permute-start | bytes 786440 | tf_op jit(solution)/shard_map/while/body/eval_jaxpr/ppermute | solution.py:16
  492.2 15.2 %collective-permute-start.2 = (bf16[2,512,128]{2,1,0:T(8,128)(2,1)S(1)}, bf16[2,512,128]{2,1,0:T(8,128)(2,1)S(1)}, u32[]{:S(2)}, u32[]{:S(2)}) collective-permute-start(bf16[2,512,128]{2,1,0:T(8,128)(2,1)S(1)} %fusion.90), channel_id=1, source_target_pairs={{124,0},{0,4},{4,8},{8,12},{12,16},{16,20},{20,24},{24,28},{28,32}... | collective-permute-start | bytes 786440 | tf_op jit(solution)/shard_map/while/body/eval_jaxpr/ppermute | solution.py:22
  508.2 20.6 %collective-permute-start.1 = (bf16[2,512,128]{2,1,0:T(8,128)(2,1)}, bf16[2,512,128]{2,1,0:T(8,128)(2,1)S(1)}, u32[]{:S(2)}, u32[]{:S(2)}) collective-permute-start(bf16[2,512,128]{2,1,0:T(8,128)(2,1)} %copy.171), channel_id=1, source_target_pairs={{0,4},{4,8},{8,12},{12,16},{16,20},{20,24},{24,28},{28,32},{32,36}... | collective-permute-start | bytes 786440 | tf_op jit(solution)/shard_map/while/body/eval_jaxpr/ppermute | solution.py:16
  513.5 15.2 %collective-permute-start.2 = (bf16[2,512,128]{2,1,0:T(8,128)(2,1)S(1)}, bf16[2,512,128]{2,1,0:T(8,128)(2,1)S(1)}, u32[]{:S(2)}, u32[]{:S(2)}) collective-permute-start(bf16[2,512,128]{2,1,0:T(8,128)(2,1)S(1)} %fusion.90), channel_id=1, source_target_pairs={{124,0},{0,4},{4,8},{8,12},{12,16},{16,20},{20,24},{24,28},{28,32}... | collective-permute-start | bytes 786440 | tf_op jit(solution)/shard_map/while/body/eval_jaxpr/ppermute | solution.py:22
  529.5 20.6 %collective-permute-start.1 = (bf16[2,512,128]{2,1,0:T(8,128)(2,1)}, bf16[2,512,128]{2,1,0:T(8,128)(2,1)S(1)}, u32[]{:S(2)}, u32[]{:S(2)}) collective-permute-start(bf16[2,512,128]{2,1,0:T(8,128)(2,1)} %copy.171), channel_id=1, source_target_pairs={{0,4},{4,8},{8,12},{12,16},{16,20},{20,24},{24,28},{28,32},{32,36}... | collective-permute-start | bytes 786440 | tf_op jit(solution)/shard_map/while/body/eval_jaxpr/ppermute | solution.py:16
  534.8 15.2 %collective-permute-start.2 = (bf16[2,512,128]{2,1,0:T(8,128)(2,1)S(1)}, bf16[2,512,128]{2,1,0:T(8,128)(2,1)S(1)}, u32[]{:S(2)}, u32[]{:S(2)}) collective-permute-start(bf16[2,512,128]{2,1,0:T(8,128)(2,1)S(1)} %fusion.90), channel_id=1, source_target_pairs={{124,0},{0,4},{4,8},{8,12},{12,16},{16,20},{20,24},{24,28},{28,32}... | collective-permute-start | bytes 786440 | tf_op jit(solution)/shard_map/while/body/eval_jaxpr/ppermute | solution.py:22
  550.8 20.6 %collective-permute-start.1 = (bf16[2,512,128]{2,1,0:T(8,128)(2,1)}, bf16[2,512,128]{2,1,0:T(8,128)(2,1)S(1)}, u32[]{:S(2)}, u32[]{:S(2)}) collective-permute-start(bf16[2,512,128]{2,1,0:T(8,128)(2,1)} %copy.171), channel_id=1, source_target_pairs={{0,4},{4,8},{8,12},{12,16},{16,20},{20,24},{24,28},{28,32},{32,36}... | collective-permute-start | bytes 786440 | tf_op jit(solution)/shard_map/while/body/eval_jaxpr/ppermute | solution.py:16
  556.1 15.2 %collective-permute-start.2 = (bf16[2,512,128]{2,1,0:T(8,128)(2,1)S(1)}, bf16[2,512,128]{2,1,0:T(8,128)(2,1)S(1)}, u32[]{:S(2)}, u32[]{:S(2)}) collective-permute-start(bf16[2,512,128]{2,1,0:T(8,128)(2,1)S(1)} %fusion.90), channel_id=1, source_target_pairs={{124,0},{0,4},{4,8},{8,12},{12,16},{16,20},{20,24},{24,28},{28,32}... | collective-permute-start | bytes 786440 | tf_op jit(solution)/shard_map/while/body/eval_jaxpr/ppermute | solution.py:22
  572.1 20.6 %collective-permute-start.1 = (bf16[2,512,128]{2,1,0:T(8,128)(2,1)}, bf16[2,512,128]{2,1,0:T(8,128)(2,1)S(1)}, u32[]{:S(2)}, u32[]{:S(2)}) collective-permute-start(bf16[2,512,128]{2,1,0:T(8,128)(2,1)} %copy.171), channel_id=1, source_target_pairs={{0,4},{4,8},{8,12},{12,16},{16,20},{20,24},{24,28},{28,32},{32,36}... | collective-permute-start | bytes 786440 | tf_op jit(solution)/shard_map/while/body/eval_jaxpr/ppermute | solution.py:16
  577.3 15.2 %collective-permute-start.2 = (bf16[2,512,128]{2,1,0:T(8,128)(2,1)S(1)}, bf16[2,512,128]{2,1,0:T(8,128)(2,1)S(1)}, u32[]{:S(2)}, u32[]{:S(2)}) collective-permute-start(bf16[2,512,128]{2,1,0:T(8,128)(2,1)S(1)} %fusion.90), channel_id=1, source_target_pairs={{124,0},{0,4},{4,8},{8,12},{12,16},{16,20},{20,24},{24,28},{28,32}... | collective-permute-start | bytes 786440 | tf_op jit(solution)/shard_map/while/body/eval_jaxpr/ppermute | solution.py:22
  593.3 13.3 %collective-permute-start.1 = (bf16[2,512,128]{2,1,0:T(8,128)(2,1)}, bf16[2,512,128]{2,1,0:T(8,128)(2,1)S(1)}, u32[]{:S(2)}, u32[]{:S(2)}) collective-permute-start(bf16[2,512,128]{2,1,0:T(8,128)(2,1)} %copy.171), channel_id=1, source_target_pairs={{0,4},{4,8},{8,12},{12,16},{16,20},{20,24},{24,28},{28,32},{32,36}... | collective-permute-start | bytes 786440 | tf_op jit(solution)/shard_map/while/body/eval_jaxpr/ppermute | solution.py:16
  607.4 13.3 %collective-permute-start.1 = (bf16[2,512,128]{2,1,0:T(8,128)(2,1)}, bf16[2,512,128]{2,1,0:T(8,128)(2,1)S(1)}, u32[]{:S(2)}, u32[]{:S(2)}) collective-permute-start(bf16[2,512,128]{2,1,0:T(8,128)(2,1)} %copy.171), channel_id=1, source_target_pairs={{0,4},{4,8},{8,12},{12,16},{16,20},{20,24},{24,28},{28,32},{32,36}... | collective-permute-start | bytes 786440 | tf_op jit(solution)/shard_map/while/body/eval_jaxpr/ppermute | solution.py:16
  621.4 13.3 %collective-permute-start.1 = (bf16[2,512,128]{2,1,0:T(8,128)(2,1)}, bf16[2,512,128]{2,1,0:T(8,128)(2,1)S(1)}, u32[]{:S(2)}, u32[]{:S(2)}) collective-permute-start(bf16[2,512,128]{2,1,0:T(8,128)(2,1)} %copy.171), channel_id=1, source_target_pairs={{0,4},{4,8},{8,12},{12,16},{16,20},{20,24},{24,28},{28,32},{32,36}... | collective-permute-start | bytes 786440 | tf_op jit(solution)/shard_map/while/body/eval_jaxpr/ppermute | solution.py:16
  635.4 13.3 %collective-permute-start.1 = (bf16[2,512,128]{2,1,0:T(8,128)(2,1)}, bf16[2,512,128]{2,1,0:T(8,128)(2,1)S(1)}, u32[]{:S(2)}, u32[]{:S(2)}) collective-permute-start(bf16[2,512,128]{2,1,0:T(8,128)(2,1)} %copy.171), channel_id=1, source_target_pairs={{0,4},{4,8},{8,12},{12,16},{16,20},{20,24},{24,28},{28,32},{32,36}... | collective-permute-start | bytes 786440 | tf_op jit(solution)/shard_map/while/body/eval_jaxpr/ppermute | solution.py:16
  649.4 13.3 %collective-permute-start.1 = (bf16[2,512,128]{2,1,0:T(8,128)(2,1)}, bf16[2,512,128]{2,1,0:T(8,128)(2,1)S(1)}, u32[]{:S(2)}, u32[]{:S(2)}) collective-permute-start(bf16[2,512,128]{2,1,0:T(8,128)(2,1)} %copy.171), channel_id=1, source_target_pairs={{0,4},{4,8},{8,12},{12,16},{16,20},{20,24},{24,28},{28,32},{32,36}... | collective-permute-start | bytes 786440 | tf_op jit(solution)/shard_map/while/body/eval_jaxpr/ppermute | solution.py:16
  663.4 13.3 %collective-permute-start.1 = (bf16[2,512,128]{2,1,0:T(8,128)(2,1)}, bf16[2,512,128]{2,1,0:T(8,128)(2,1)S(1)}, u32[]{:S(2)}, u32[]{:S(2)}) collective-permute-start(bf16[2,512,128]{2,1,0:T(8,128)(2,1)} %copy.171), channel_id=1, source_target_pairs={{0,4},{4,8},{8,12},{12,16},{16,20},{20,24},{24,28},{28,32},{32,36}... | collective-permute-start | bytes 786440 | tf_op jit(solution)/shard_map/while/body/eval_jaxpr/ppermute | solution.py:16
  677.4 13.3 %collective-permute-start.1 = (bf16[2,512,128]{2,1,0:T(8,128)(2,1)}, bf16[2,512,128]{2,1,0:T(8,128)(2,1)S(1)}, u32[]{:S(2)}, u32[]{:S(2)}) collective-permute-start(bf16[2,512,128]{2,1,0:T(8,128)(2,1)} %copy.171), channel_id=1, source_target_pairs={{0,4},{4,8},{8,12},{12,16},{16,20},{20,24},{24,28},{28,32},{32,36}... | collective-permute-start | bytes 786440 | tf_op jit(solution)/shard_map/while/body/eval_jaxpr/ppermute | solution.py:16
  691.5 13.3 %collective-permute-start.1 = (bf16[2,512,128]{2,1,0:T(8,128)(2,1)}, bf16[2,512,128]{2,1,0:T(8,128)(2,1)S(1)}, u32[]{:S(2)}, u32[]{:S(2)}) collective-permute-start(bf16[2,512,128]{2,1,0:T(8,128)(2,1)} %copy.171), channel_id=1, source_target_pairs={{0,4},{4,8},{8,12},{12,16},{16,20},{20,24},{24,28},{28,32},{32,36}... | collective-permute-start | bytes 786440 | tf_op jit(solution)/shard_map/while/body/eval_jaxpr/ppermute | solution.py:16
  705.5 13.3 %collective-permute-start.1 = (bf16[2,512,128]{2,1,0:T(8,128)(2,1)}, bf16[2,512,128]{2,1,0:T(8,128)(2,1)S(1)}, u32[]{:S(2)}, u32[]{:S(2)}) collective-permute-start(bf16[2,512,128]{2,1,0:T(8,128)(2,1)} %copy.171), channel_id=1, source_target_pairs={{0,4},{4,8},{8,12},{12,16},{16,20},{20,24},{24,28},{28,32},{32,36}... | collective-permute-start | bytes 786440 | tf_op jit(solution)/shard_map/while/body/eval_jaxpr/ppermute | solution.py:16
  719.5 13.3 %collective-permute-start.1 = (bf16[2,512,128]{2,1,0:T(8,128)(2,1)}, bf16[2,512,128]{2,1,0:T(8,128)(2,1)S(1)}, u32[]{:S(2)}, u32[]{:S(2)}) collective-permute-start(bf16[2,512,128]{2,1,0:T(8,128)(2,1)} %copy.171), channel_id=1, source_target_pairs={{0,4},{4,8},{8,12},{12,16},{16,20},{20,24},{24,28},{28,32},{32,36}... | collective-permute-start | bytes 786440 | tf_op jit(solution)/shard_map/while/body/eval_jaxpr/ppermute | solution.py:16
  733.5 13.3 %collective-permute-start.1 = (bf16[2,512,128]{2,1,0:T(8,128)(2,1)}, bf16[2,512,128]{2,1,0:T(8,128)(2,1)S(1)}, u32[]{:S(2)}, u32[]{:S(2)}) collective-permute-start(bf16[2,512,128]{2,1,0:T(8,128)(2,1)} %copy.171), channel_id=1, source_target_pairs={{0,4},{4,8},{8,12},{12,16},{16,20},{20,24},{24,28},{28,32},{32,36}... | collective-permute-start | bytes 786440 | tf_op jit(solution)/shard_map/while/body/eval_jaxpr/ppermute | solution.py:16
  747.5 13.3 %collective-permute-start.1 = (bf16[2,512,128]{2,1,0:T(8,128)(2,1)}, bf16[2,512,128]{2,1,0:T(8,128)(2,1)S(1)}, u32[]{:S(2)}, u32[]{:S(2)}) collective-permute-start(bf16[2,512,128]{2,1,0:T(8,128)(2,1)} %copy.171), channel_id=1, source_target_pairs={{0,4},{4,8},{8,12},{12,16},{16,20},{20,24},{24,28},{28,32},{32,36}... | collective-permute-start | bytes 786440 | tf_op jit(solution)/shard_map/while/body/eval_jaxpr/ppermute | solution.py:16
  761.6 13.3 %collective-permute-start.1 = (bf16[2,512,128]{2,1,0:T(8,128)(2,1)}, bf16[2,512,128]{2,1,0:T(8,128)(2,1)S(1)}, u32[]{:S(2)}, u32[]{:S(2)}) collective-permute-start(bf16[2,512,128]{2,1,0:T(8,128)(2,1)} %copy.171), channel_id=1, source_target_pairs={{0,4},{4,8},{8,12},{12,16},{16,20},{20,24},{24,28},{28,32},{32,36}... | collective-permute-start | bytes 786440 | tf_op jit(solution)/shard_map/while/body/eval_jaxpr/ppermute | solution.py:16
  775.6 13.3 %collective-permute-start.1 = (bf16[2,512,128]{2,1,0:T(8,128)(2,1)}, bf16[2,512,128]{2,1,0:T(8,128)(2,1)S(1)}, u32[]{:S(2)}, u32[]{:S(2)}) collective-permute-start(bf16[2,512,128]{2,1,0:T(8,128)(2,1)} %copy.171), channel_id=1, source_target_pairs={{0,4},{4,8},{8,12},{12,16},{16,20},{20,24},{24,28},{28,32},{32,36}... | collective-permute-start | bytes 786440 | tf_op jit(solution)/shard_map/while/body/eval_jaxpr/ppermute | solution.py:16
  789.6 13.3 %collective-permute-start.1 = (bf16[2,512,128]{2,1,0:T(8,128)(2,1)}, bf16[2,512,128]{2,1,0:T(8,128)(2,1)S(1)}, u32[]{:S(2)}, u32[]{:S(2)}) collective-permute-start(bf16[2,512,128]{2,1,0:T(8,128)(2,1)} %copy.171), channel_id=1, source_target_pairs={{0,4},{4,8},{8,12},{12,16},{16,20},{20,24},{24,28},{28,32},{32,36}... | collective-permute-start | bytes 786440 | tf_op jit(solution)/shard_map/while/body/eval_jaxpr/ppermute | solution.py:16
  803.6 13.3 %collective-permute-start.1 = (bf16[2,512,128]{2,1,0:T(8,128)(2,1)}, bf16[2,512,128]{2,1,0:T(8,128)(2,1)S(1)}, u32[]{:S(2)}, u32[]{:S(2)}) collective-permute-start(bf16[2,512,128]{2,1,0:T(8,128)(2,1)} %copy.171), channel_id=1, source_target_pairs={{0,4},{4,8},{8,12},{12,16},{16,20},{20,24},{24,28},{28,32},{32,36}... | collective-permute-start | bytes 786440 | tf_op jit(solution)/shard_map/while/body/eval_jaxpr/ppermute | solution.py:16
  817.6 13.3 %collective-permute-start.1 = (bf16[2,512,128]{2,1,0:T(8,128)(2,1)}, bf16[2,512,128]{2,1,0:T(8,128)(2,1)S(1)}, u32[]{:S(2)}, u32[]{:S(2)}) collective-permute-start(bf16[2,512,128]{2,1,0:T(8,128)(2,1)} %copy.171), channel_id=1, source_target_pairs={{0,4},{4,8},{8,12},{12,16},{16,20},{20,24},{24,28},{28,32},{32,36}... | collective-permute-start | bytes 786440 | tf_op jit(solution)/shard_map/while/body/eval_jaxpr/ppermute | solution.py:16
  831.6 13.3 %collective-permute-start.1 = (bf16[2,512,128]{2,1,0:T(8,128)(2,1)}, bf16[2,512,128]{2,1,0:T(8,128)(2,1)S(1)}, u32[]{:S(2)}, u32[]{:S(2)}) collective-permute-start(bf16[2,512,128]{2,1,0:T(8,128)(2,1)} %copy.171), channel_id=1, source_target_pairs={{0,4},{4,8},{8,12},{12,16},{16,20},{20,24},{24,28},{28,32},{32,36}... | collective-permute-start | bytes 786440 | tf_op jit(solution)/shard_map/while/body/eval_jaxpr/ppermute | solution.py:16
  845.7 13.3 %collective-permute-start.1 = (bf16[2,512,128]{2,1,0:T(8,128)(2,1)}, bf16[2,512,128]{2,1,0:T(8,128)(2,1)S(1)}, u32[]{:S(2)}, u32[]{:S(2)}) collective-permute-start(bf16[2,512,128]{2,1,0:T(8,128)(2,1)} %copy.171), channel_id=1, source_target_pairs={{0,4},{4,8},{8,12},{12,16},{16,20},{20,24},{24,28},{28,32},{32,36}... | collective-permute-start | bytes 786440 | tf_op jit(solution)/shard_map/while/body/eval_jaxpr/ppermute | solution.py:16
  859.7 13.3 %collective-permute-start.1 = (bf16[2,512,128]{2,1,0:T(8,128)(2,1)}, bf16[2,512,128]{2,1,0:T(8,128)(2,1)S(1)}, u32[]{:S(2)}, u32[]{:S(2)}) collective-permute-start(bf16[2,512,128]{2,1,0:T(8,128)(2,1)} %copy.171), channel_id=1, source_target_pairs={{0,4},{4,8},{8,12},{12,16},{16,20},{20,24},{24,28},{28,32},{32,36}... | collective-permute-start | bytes 786440 | tf_op jit(solution)/shard_map/while/body/eval_jaxpr/ppermute | solution.py:16
  873.7 13.3 %collective-permute-start.1 = (bf16[2,512,128]{2,1,0:T(8,128)(2,1)}, bf16[2,512,128]{2,1,0:T(8,128)(2,1)S(1)}, u32[]{:S(2)}, u32[]{:S(2)}) collective-permute-start(bf16[2,512,128]{2,1,0:T(8,128)(2,1)} %copy.171), channel_id=1, source_target_pairs={{0,4},{4,8},{8,12},{12,16},{16,20},{20,24},{24,28},{28,32},{32,36}... | collective-permute-start | bytes 786440 | tf_op jit(solution)/shard_map/while/body/eval_jaxpr/ppermute | solution.py:16
  887.7 13.3 %collective-permute-start.1 = (bf16[2,512,128]{2,1,0:T(8,128)(2,1)}, bf16[2,512,128]{2,1,0:T(8,128)(2,1)S(1)}, u32[]{:S(2)}, u32[]{:S(2)}) collective-permute-start(bf16[2,512,128]{2,1,0:T(8,128)(2,1)} %copy.171), channel_id=1, source_target_pairs={{0,4},{4,8},{8,12},{12,16},{16,20},{20,24},{24,28},{28,32},{32,36}... | collective-permute-start | bytes 786440 | tf_op jit(solution)/shard_map/while/body/eval_jaxpr/ppermute | solution.py:16
  912.6 9.9 %all-to-all-start.7 = ((bf16[4,128,128]{2,1,0:T(8,128)(2,1)}), bf16[4,128,128]{2,1,0:T(8,128)(2,1)S(1)}, u32[]{:S(2)}, u32[]{:S(2)}) async-start(bf16[4,128,128]{2,1,0:T(8,128)(2,1)} %bitcast.78), calls=%async_computation.7 | async-start | bytes 262144 | tf_op jit(solution)/shard_map/all_to_all | solution.py:214
  922.5 14.5 %all-to-all-start.5 = ((bf16[4,128,640]{1,2,0:T(8,128)(2,1)}), bf16[4,128,640]{1,2,0:T(8,128)(2,1)S(1)}, u32[]{:S(2)}, u32[]{:S(2)}) async-start(bf16[4,128,640]{1,2,0:T(8,128)(2,1)} %copy.124), calls=%async_computation.5 | async-start | bytes 1310720 | tf_op jit(solution)/shard_map/all_to_all | solution.py:204
  937.0 12.2 %all-to-all-start.3 = ((bf16[4,128,640]{1,2,0:T(8,128)(2,1)}), bf16[4,128,640]{1,2,0:T(8,128)(2,1)S(1)}, u32[]{:S(2)}, u32[]{:S(2)}) async-start(bf16[4,128,640]{1,2,0:T(8,128)(2,1)} %copy.118), calls=%async_computation.3 | async-start | bytes 1310720 | tf_op jit(solution)/shard_map/all_to_all | solution.py:201
  (59 other events, 521.0 us)
where the time goes:
time: 958 us; the launch traced here: 950 us
  waiting for transfers between devices  387 us (40%)
  other arithmetic  248 us (26%)
  starting transfers between devices  172 us (18%)
  local copies, waits for them, and re-layouts  53.7 us (6%)
  loops' own time  46.5 us (5%)
  matrix products  30.4 us (3%)
  blocking collectives  10.8 us (1%)
    ppermute x32, waiting for transfers between devices, passed_along_2(): return lax.ppermute(block, axis, route)  197 us
    ppermute x63, waiting for transfers between devices, passed_along(): return lax.ppermute(value, axis, pairs)  162 us
    ppermute x63, starting transfers between devices, passed_along(): return lax.ppermute(value, axis, pairs)  133 us
    add x32, other arithmetic, backward_advance(): return (query_inner + query_part, sums_inner)  80.8 us
    reduce_or x32, other arithmetic, backward_advance(): query_part, key_value_part = lax.cond(jnp.any(visible), compute, nothing, 0)  55 us
    reduce_or x31, other arithmetic, sweep_advance(): jnp.any(visible)  52.3 us
    reduce_sum x64, other arithmetic, placed(): jnp.sum((position[:, None] >= doc_ends[None, :]).astype(jnp.int32), axis=1)  46.3 us
    another operation x1, loops' own time, per_device(): lax.fori_loop(0, seq_count, backward_turn, (start_query, key_value, start...  23.7 us
  transfers between devices with their start and end apart: 102, of which 68 were waited for; matrix products, arithmetic and copies ran while one was open for 31% of the time, Pallas kernels for 0%

commit v1 on v0

--- a/solution.py
+++ b/solution.py
@@ -8,18 +8,17 @@
 HD = 128
 QH = 20
 KVH = 4
-
-
-def passed_along(value, axis, by):
+LONG = 4096
+
+
+def shifted(value, axis, by):
     peers = lax.axis_size(axis)
     pairs = [(i, i + by) for i in range(peers) if 0 <= i + by < peers]
     return lax.ppermute(value, axis, pairs)
 
 
-def passed_along_2(block, axis, distance):
-    devices = range(lax.axis_size(axis))
-    route = [((i - distance) % len(devices), i) for i in devices]
-    return lax.ppermute(block, axis, route)
+def segment_of(position, doc_ends):
+    return jnp.sum((position >= doc_ends).astype(jnp.int32))
 
 
 def placed(first_row, row_count, doc_ends):
@@ -102,101 +101,75 @@
     seq_count = lax.axis_size("seq")
     position = lax.axis_index("seq")
     doc_ends = jnp.cumsum(doc_lengths)
-    query_pos, query_seg = placed(position * length, length, doc_ends)
-    span_rows = math.gcd(length, 512)
-
-    def sweep_keys(softmax_state, key_piece, value_piece, first_row):
-
-        def sweep_advance(block_index, current):
-            offset = block_index * span_rows
-            key_block = key_piece.reshape(span_rows, kv_heads, HD)
-            value_block = value_piece.reshape(span_rows, kv_heads, HD)
-            key_pos, key_seg = placed(first_row + offset, span_rows, doc_ends)
-            visible = allowed(query_pos, query_seg, key_pos, key_seg)
-            return lax.cond(
-                jnp.any(visible),
-                lambda carried: absorb(
-                    carried, query_heads, key_block, value_block, visible, scaling
-                ),
-                lambda carried: carried,
-                current,
-            )
-
-        return lax.fori_loop(0, length // span_rows, sweep_advance, softmax_state)
-
-    initial = (
+    first_query = position * length
+    query_pos, query_seg = placed(first_query, length, doc_ends)
+    first_seg = segment_of(first_query, doc_ends)
+    reach = min((length - 1 + LONG - 1) // length, seq_count - 1)
+
+    key_value = jnp.stack((key_here, value_here))
+    gathered = [key_value] + [shifted(key_value, "seq", d) for d in range(1, reach + 1)]
+
+    def block_mask(d):
+        first_key = first_query - d * length
+        key_pos, key_seg = placed(first_key, length, doc_ends)
+        visible = allowed(query_pos, query_seg, key_pos, key_seg)
+        if d == 0:
+            live = jnp.bool_(True)
+        else:
+            last_key = first_key + length - 1
+            live = (last_key >= 0) & (segment_of(last_key, doc_ends) == first_seg)
+        return visible, live
+
+    softmax_state = (
         jnp.full((length, kv_heads, per_kv), -1e30, jnp.float32),
         jnp.zeros((length, kv_heads, per_kv), jnp.float32),
         jnp.zeros((length, kv_heads, per_kv, HD), jnp.float32),
     )
-    softmax_state = sweep_keys(initial, key_here, value_here, position * length)
-
-    def travel(turn_index, carried):
-        current, key_value = carried
-        key_value = passed_along(key_value, "seq", 1)
-        current = sweep_keys(current, key_value[0], key_value[1], (position - turn_index) * length)
-        return (current, key_value)
-
-    softmax_state, spent = lax.fori_loop(
-        1, seq_count, travel, (softmax_state, jnp.stack((key_here, value_here)))
-    )
+    for d in range(reach + 1):
+        visible, live = block_mask(d)
+        key_block = gathered[d][0].reshape(length, kv_heads, HD)
+        value_block = gathered[d][1].reshape(length, kv_heads, HD)
+        softmax_state = lax.cond(
+            live,
+            lambda carried, kb=key_block, vb=value_block, vis=visible: absorb(
+                carried, query_heads, kb, vb, vis, scaling
+            ),
+            lambda carried: carried,
+            softmax_state,
+        )
     running, denominator, accumulated = softmax_state
     out_heads = (accumulated / denominator[..., None]).astype(jnp.bfloat16)
     log_total = running + jnp.log(denominator)
     row_dot = jnp.sum(grad_heads.astype(jnp.float32) * out_heads.astype(jnp.float32), axis=-1)
 
-    def backward_turn(turn_index, carried):
-        query_acc, key_value, grad_sums = carried
-        source_shard = (position - turn_index) % seq_count
-
-        def backward_advance(block_index, inner_carry):
-            query_inner, sums_inner = inner_carry
-            offset = block_index * span_rows
-            key_block = key_value[0].reshape(span_rows, kv_heads, HD)
-            value_block = key_value[1].reshape(span_rows, kv_heads, HD)
-            key_pos, key_seg = placed(source_shard * length + offset, span_rows, doc_ends)
-            visible = allowed(query_pos, query_seg, key_pos, key_seg)
-
-            def compute(unused):
-                query_part, key_part, value_part = contrib(
-                    query_heads,
-                    grad_heads,
-                    log_total,
-                    row_dot,
-                    key_block,
-                    value_block,
-                    visible,
-                    scaling,
-                )
-                return (
-                    query_part,
-                    jnp.stack((key_part.reshape(span_rows, -1), value_part.reshape(span_rows, -1))),
-                )
-
-            def nothing(unused):
-                return (
-                    jnp.zeros_like(query_inner),
-                    jnp.zeros((2, span_rows, key_value.shape[2]), jnp.float32),
-                )
-
-            query_part, key_value_part = lax.cond(jnp.any(visible), compute, nothing, 0)
-            current = sums_inner
-            sums_inner = current + key_value_part
-            return (query_inner + query_part, sums_inner)
-
-        query_acc, grad_sums = lax.fori_loop(
-            0, length // span_rows, backward_advance, (query_acc, grad_sums)
-        )
-        key_value = passed_along(key_value, "seq", 1)
-        grad_sums = passed_along_2(grad_sums.astype(jnp.bfloat16), "seq", 1).astype(grad_sums.dtype)
-        return (query_acc, key_value, grad_sums)
-
-    key_value = jnp.stack((key_here, value_here))
-    start_sums = jnp.zeros(key_value.shape, jnp.float32)
-    start_query = jnp.zeros((length, kv_heads, per_kv, HD), jnp.float32)
-    query_acc, spent_pair, grad_sums = lax.fori_loop(
-        0, seq_count, backward_turn, (start_query, key_value, start_sums)
-    )
+    query_acc = jnp.zeros((length, kv_heads, per_kv, HD), jnp.float32)
+    grad_sums = None
+    for d in range(reach + 1):
+        visible, live = block_mask(d)
+        key_block = gathered[d][0].reshape(length, kv_heads, HD)
+        value_block = gathered[d][1].reshape(length, kv_heads, HD)
+
+        def compute(unused, kb=key_block, vb=value_block, vis=visible):
+            query_part, key_part, value_part = contrib(
+                query_heads, grad_heads, log_total, row_dot, kb, vb, vis, scaling
+            )
+            return (
+                query_part,
+                jnp.stack((key_part.reshape(length, -1), value_part.reshape(length, -1))),
+            )
+
+        def nothing(unused):
+            return (
+                jnp.zeros((length, kv_heads, per_kv, HD), jnp.float32),
+                jnp.zeros((2, length, kv_heads * HD), jnp.float32),
+            )
+
+        query_part, key_value_part = lax.cond(live, compute, nothing, 0)
+        query_acc = query_acc + query_part
+        if d > 0:
+            key_value_part = shifted(key_value_part, "seq", -d)
+        grad_sums = key_value_part if grad_sums is None else grad_sums + key_value_part
+
     outputs = (
         lax.all_to_all(
             out_heads.reshape(length, -1), "tp", split_axis=0, concat_axis=1, tiled=True

time: 958 us -> 299 us (0.31)
  waiting for transfers between devices: 387 us -> 37.9 us
  other arithmetic: 248 us -> 32 us
  starting transfers between devices: 172 us -> 72.4 us
  matrix products: 30.4 us -> 111 us
  loops' own time: 46.5 us -> 3.3 us
  local copies, waits for them, and re-layouts: 53.7 us -> 29.5 us
  blocking collectives: 10.8 us -> 0 us
  between operations: 1.5 us -> 11.5 us
    ppermute x95 -> x16, waiting for transfers between devices: 359 us -> 23.3 us  [shifted(): return lax.ppermute(value, axis, pairs)]
    ppermute x95 -> x16, starting transfers between devices: 146 us -> 38.1 us  [shifted(): return lax.ppermute(value, axis, pairs)]
    reduce_or x63 -> x0, other arithmetic: 107 us -> none  [the longest x32 55 us: backward_advance(): query_part, key_value_part = lax.cond(jnp.any(visible), compute, nothing, 0)]
    add x32 -> x0, other arithmetic: 80.8 us -> none  [backward_advance(): return (query_inner + query_part, sums_inner)]
    reduce_sum x64 -> x1, other arithmetic: 46.3 us -> 0.13 us  [placed(): jnp.sum((position[:, None] >= doc_ends[None, :]).astype(jnp.int32), axis=1)]
    another operation x66 -> x16, loops' own time: 46.5 us -> 3.3 us  [the longest x8 2.01 us: per_device(): query_part, key_value_part = lax.cond(live, compute, nothing, 0)]
    while x64 -> x0, local copies, waits for them, and re-layouts: 24.4 us -> none
    dot_general x2 -> x9, matrix products: 9.56 us -> 33.8 us  [absorb(): jnp.einsum('bkgt,tkd->bkgd', weight.astype(jnp.bfloat16), value_block, pr...]
  transfers between devices with their start and end apart: 102 -> 24, of which waited for: 68 -> 10; matrix products, arithmetic and copies ran while one was open for 31% -> 35% of each run, Pallas kernels for 0% -> 0%
where the time goes in v1:
time: 299 us; the launch traced here: 297 us
  matrix products  111 us (37%)
  starting transfers between devices  72.4 us (24%)
  waiting for transfers between devices  37.9 us (13%)
  other arithmetic  32 us (11%)
  local copies, waits for them, and re-layouts  29.5 us (10%)
  between operations  11.5 us (4%)
  loops' own time  3.3 us (1%)
    ppermute x16, starting transfers between devices, shifted(): return lax.ppermute(value, axis, pairs)  38.1 us
    dot_general x9, matrix products, absorb(): jnp.einsum('bkgt,tkd->bkgd', weight.astype(jnp.bfloat16), value_block, pr...  33.8 us
    ppermute x16, waiting for transfers between devices, shifted(): return lax.ppermute(value, axis, pairs)  23.3 us
    dot_general x9, matrix products, contrib(): jnp.einsum('bkgd,tkd->bkgt', grad_heads, value_block, preferred_element_t...  21.1 us
    dot_general x9, matrix products, contrib(): jnp.einsum('bkgt,bkgd->tkd', probability.astype(jnp.bfloat16), grad_heads...  17.1 us
    reduce_sum x9, other arithmetic, absorb(): denominator = denominator * shrink + jnp.sum(weight, axis=-1)  11.4 us
    unnamed x106, local copies, waits for them, and re-layouts  11.1 us
    dot_general x9, matrix products, contrib(): jnp.einsum('bkgt,bkgd->tkd', grad_score, query_heads, preferred_element_t...  10.1 us
  transfers between devices with their start and end apart: 24, of which 10 were waited for; matrix products, arithmetic and copies ran while one was open for 35% of the time, Pallas kernels for 0%

profile of v1, /device:TPU:16, one launch (start us, length us, event | category | flops | bytes accessed | tf_op | source)
XLA Modules:
  0.0 297.4 jit_solution(16846709707397339767)
XLA Ops:
  2.2 4.3 %all-to-all-start = ((bf16[128,4,128]{2,0,1:T(8,128)(2,1)}), bf16[128,4,128]{2,0,1:T(8,128)(2,1)S(1)}, u32[]{:S(2)}, u32[]{:S(2)}) async-start(bf16[128,4,128]{2,0,1:T(8,128)(2,1)} %copy_bitcast_fusion.3), calls=%async_computation | async-start | bytes 262144 | tf_op jit(solution)/shard_map/all_to_all | solution.py:93
  11.3 4.1 %compare_and_fusion = (pred[512,512]{0,1:T(8,128)(4,1)}, pred[512,512]{0,1:T(8,128)(4,1)}, pred[512,512]{0,1:T(8,128)(4,1)}, pred[512,512]{0,1:T(8,128)(4,1)}, p...) fusion(s32[512]{0:T(512)S(1)} %get-tuple-element.958, s32[512]{0:T(512)S(1)} %iota_add_fusion.8, ...), kind=kLoop, calls=%fused_computation.440 | loop fusion | flops 6291456 | bytes 1600512 | tf_op jit(solution)/shard_map/and | solution.py:32
  15.4 4.8 %all-to-all-start.2 = ((bf16[128,4,128]{2,0,1:T(8,128)(2,1)}), bf16[128,4,128]{2,0,1:T(8,128)(2,1)S(1)}, u32[]{:S(2)}, u32[]{:S(2)}) async-start(bf16[128,4,128]{2,0,1:T(8,128)(2,1)} %copy_bitcast_fusion.2), calls=%async_computation.2 | async-start | bytes 262144 | tf_op jit(solution)/shard_map/all_to_all | solution.py:94
  20.3 6.0 %all-to-all-done.2 = bf16[128,4,128]{2,0,1:T(8,128)(2,1)S(1)} async-done(((bf16[128,4,128]{2,0,1:T(8,128)(2,1)}), bf16[128,4,128]{2,0,1:T(8,128)(2,1)S(1)}, u32[]{:S(2)}, u32[]{:S(2)}) %all-to-all-start.2) | async-done | bytes 131104 | tf_op jit(solution)/shard_map/all_to_all | solution.py:94
  26.2 3.5 %all-to-all-start.1 = ((bf16[128,4,640]{0,2,1:T(8,128)(2,1)}), bf16[128,4,640]{0,2,1:T(8,128)(2,1)S(1)}, u32[]{:S(2)}, u32[]{:S(2)}) async-start(bf16[128,4,640]{0,2,1:T(8,128)(2,1)} %bitcast.341), calls=%async_computation.1 | async-start | bytes 1310720 | tf_op jit(solution)/shard_map/all_to_all | solution.py:92
  29.8 3.2 %collective-permute-start.7 = (bf16[2,512,128]{2,1,0:T(8,128)(2,1)S(1)}, bf16[2,512,128]{2,1,0:T(8,128)(2,1)S(1)}, u32[]{:S(2)}, u32[]{:S(2)}) collective-permute-start(bf16[2,512,128]{2,1,0:T(8,128)(2,1)S(1)} %pad_maximum_fusion.8), channel_id=1, source_target_pairs={{0,32},{4,36},{8,40},{12,44},{16,48},{20,52},{24,56},{28,60},{32,6... | collective-permute-start | bytes 786440 | tf_op jit(solution)/shard_map/ppermute | solution.py:17
  34.2 3.1 %collective-permute-start.6 = (bf16[2,512,128]{2,1,0:T(8,128)(2,1)S(1)}, bf16[2,512,128]{2,1,0:T(8,128)(2,1)S(1)}, u32[]{:S(2)}, u32[]{:S(2)}) collective-permute-start(bf16[2,512,128]{2,1,0:T(8,128)(2,1)S(1)} %pad_maximum_fusion.8), channel_id=1, source_target_pairs={{0,28},{4,32},{8,36},{12,40},{16,44},{20,48},{24,52},{28,56},{32,6... | collective-permute-start | bytes 786440 | tf_op jit(solution)/shard_map/ppermute | solution.py:17
  48.8 4.7 %collective-permute-start.5 = (bf16[2,512,128]{2,1,0:T(8,128)(2,1)S(1)}, bf16[2,512,128]{2,1,0:T(8,128)(2,1)S(1)}, u32[]{:S(2)}, u32[]{:S(2)}) collective-permute-start(bf16[2,512,128]{2,1,0:T(8,128)(2,1)S(1)} %pad_maximum_fusion.8), channel_id=1, source_target_pairs={{0,24},{4,28},{8,32},{12,36},{16,40},{20,44},{24,48},{28,52},{32,5... | collective-permute-start | bytes 786440 | tf_op jit(solution)/shard_map/ppermute | solution.py:17
  63.6 2.9 collective-permute-start
  67.9 5.0 %collective-permute-done.3 = bf16[2,512,128]{2,1,0:T(8,128)(2,1)S(1)} collective-permute-done((bf16[2,512,128]{2,1,0:T(8,128)(2,1)S(1)}, bf16[2,512,128]{2,1,0:T(8,128)(2,1)S(1)}, u32[]{:S(2)}, u32[]{:S(2)}) %collective-permute-start.3) | collective-permute-done | bytes 262176 | tf_op jit(solution)/shard_map/ppermute | solution.py:17
  73.6 4.8 %all-to-all-start.4 = ((bf16[128,4,640]{0,2,1:T(8,128)(2,1)}), bf16[128,4,640]{0,2,1:T(8,128)(2,1)S(1)}, u32[]{:S(2)}, u32[]{:S(2)}) async-start(bf16[128,4,640]{0,2,1:T(8,128)(2,1)} %bitcast.378), calls=%async_computation.4 | async-start | bytes 1310720 | tf_op jit(solution)/shard_map/all_to_all | solution.py:95
  79.1 5.3 %collective-permute-done.1 = bf16[2,512,128]{2,1,0:T(8,128)(2,1)S(1)} collective-permute-done((bf16[2,512,128]{2,1,0:T(8,128)(2,1)S(1)}, bf16[2,512,128]{2,1,0:T(8,128)(2,1)S(1)}, u32[]{:S(2)}, u32[]{:S(2)}) %collective-permute-start.1) | collective-permute-done | bytes 262176 | tf_op jit(solution)/shard_map/ppermute | solution.py:17
  94.6 2.8 fusion.406
  97.4 6.7 %conditional.16 = ((f32[512,1,5]{0,2,1:T(8,128)S(1)}, f32[512,1,5]{0,2,1:T(8,128)S(1)}, f32[512,1,5,128]{3,0,2,1:T(8,128)})) conditional(s32[]{:T(128)} %convert_element_type.231, (f32[512,1,5]{0,2,1:T(8,128)S(1)}, f32[512,1,5]{0,2,1:T(8,128)S(1)}, f32[512,1,5,128]{3,0,2,1:T(8,128)}) %tuple.121, (pred[512,512]{0,1:T(8,128)(4,1)S(1)}, ...), branch_computations={%region_14.15_spmd, %region_15.18_spmd} | conditional | flops 688791040 | bytes 20217888 | solution.py:132
  99.0 3.9 %fusion.10 = f32[512,1,5,128]{3,0,2,1:T(8,128)} fusion(f32[512,512,5]{1,0,2:T(8,128)S(1)} %get-tuple-element.987, f32[512,5]{0,1:T(8,128)S(1)} %bitcast.1501, pred[512,512]{0,1:T(8,128)(4,1)S(1)} %get-tuple-element.273, f32[512,1,5,128]{3,0,2,1:T(8,128)} %get-tuple-element.277, f32[512,5]{0,1:T(8,128)S(1)} %get-tuple-element.968, ...), kind=kOutput, calls=%fused_computation.9 | convolution fusion | flops 342753280 | bytes 8278016 | tf_op jit(solution)/shard_map/cond/branch_1_fun/bkgt,tkd->bkgd/dot_general | solution.py:50
  104.2 6.2 %conditional.17 = ((f32[512,1,5]{0,2,1:T(8,128)S(1)}, f32[512,1,5]{0,2,1:T(8,128)S(1)}, f32[512,1,5,128]{3,0,2,1:T(8,128)})) conditional(s32[]{:T(128)} %convert_element_type.229, (f32[512,1,5]{0,2,1:T(8,128)S(1)}, f32[512,1,5]{0,2,1:T(8,128)S(1)}, f32[512,1,5,128]{3,0,2,1:T(8,128)}) %get-tuple-element.1132, (pred[512,512]{0,1:T(8,128)(4,1)S(1)}, ...), branch_computations={%region_19.20_spmd, %region_20.23_spmd} | conditional | flops 688791040 | bytes 20217888 | solution.py:132
  105.3 3.9 %fusion.31 = f32[512,1,5,128]{3,0,2,1:T(8,128)} fusion(f32[512,512,5]{1,0,2:T(8,128)S(1)} %get-tuple-element.989, f32[512,5]{0,1:T(8,128)S(1)} %bitcast.1503, pred[512,512]{0,1:T(8,128)(4,1)S(1)} %get-tuple-element.280, f32[512,1,5,128]{3,0,2,1:T(8,128)} %get-tuple-element.284, f32[512,5]{0,1:T(8,128)S(1)} %get-tuple-element.970, ...), kind=kOutput, calls=%fused_computation.30 | convolution fusion | flops 342753280 | bytes 8278016 | tf_op jit(solution)/shard_map/cond/branch_1_fun/bkgt,tkd->bkgd/dot_general | solution.py:50
  110.5 6.2 %conditional.18 = ((f32[512,1,5]{0,2,1:T(8,128)S(1)}, f32[512,1,5]{0,2,1:T(8,128)S(1)}, f32[512,1,5,128]{3,0,2,1:T(8,128)})) conditional(s32[]{:T(128)} %convert_element_type.227, (f32[512,1,5]{0,2,1:T(8,128)S(1)}, f32[512,1,5]{0,2,1:T(8,128)S(1)}, f32[512,1,5,128]{3,0,2,1:T(8,128)}) %get-tuple-element.1133, (pred[512,512]{0,1:T(8,128)(4,1)S(1)}, ...), branch_computations={%region_24.25_spmd, %region_25.28_spmd} | conditional | flops 688791040 | bytes 20217888 | solution.py:132
  111.6 3.9 %fusion.52 = f32[512,1,5,128]{3,0,2,1:T(8,128)} fusion(f32[512,512,5]{1,0,2:T(8,128)S(1)} %get-tuple-element.991, f32[512,5]{0,1:T(8,128)S(1)} %bitcast.1505, pred[512,512]{0,1:T(8,128)(4,1)S(1)} %get-tuple-element.287, f32[512,1,5,128]{3,0,2,1:T(8,128)} %get-tuple-element.291, f32[512,5]{0,1:T(8,128)S(1)} %get-tuple-element.972, ...), kind=kOutput, calls=%fused_computation.51 | convolution fusion | flops 342753280 | bytes 8278016 | tf_op jit(solution)/shard_map/cond/branch_1_fun/bkgt,tkd->bkgd/dot_general | solution.py:50
  116.8 6.4 %conditional.19 = ((f32[512,1,5]{0,2,1:T(8,128)S(1)}, f32[512,1,5]{0,2,1:T(8,128)S(1)}, f32[512,1,5,128]{3,0,2,1:T(8,128)})) conditional(s32[]{:T(128)} %convert_element_type.225, (f32[512,1,5]{0,2,1:T(8,128)S(1)}, f32[512,1,5]{0,2,1:T(8,128)S(1)}, f32[512,1,5,128]{3,0,2,1:T(8,128)}) %get-tuple-element.1134, (pred[512,512]{0,1:T(8,128)(4,1)S(1)}, ...), branch_computations={%region_29.30_spmd, %region_30.33_spmd} | conditional | flops 688791040 | bytes 20217888 | solution.py:132
  118.0 3.9 %fusion.73 = f32[512,1,5,128]{3,0,2,1:T(8,128)} fusion(f32[512,512,5]{1,0,2:T(8,128)S(1)} %get-tuple-element.993, f32[512,5]{0,1:T(8,128)S(1)} %bitcast.1507, pred[512,512]{0,1:T(8,128)(4,1)S(1)} %get-tuple-element.294, f32[512,1,5,128]{3,0,2,1:T(8,128)} %get-tuple-element.298, f32[512,5]{0,1:T(8,128)S(1)} %get-tuple-element.974, ...), kind=kOutput, calls=%fused_computation.72 | convolution fusion | flops 342753280 | bytes 8278016 | tf_op jit(solution)/shard_map/cond/branch_1_fun/bkgt,tkd->bkgd/dot_general | solution.py:50
  123.2 6.2 %conditional.20 = ((f32[512,1,5]{0,2,1:T(8,128)S(1)}, f32[512,1,5]{0,2,1:T(8,128)S(1)}, f32[512,1,5,128]{3,0,2,1:T(8,128)})) conditional(s32[]{:T(128)} %convert_element_type.223, (f32[512,1,5]{0,2,1:T(8,128)S(1)}, f32[512,1,5]{0,2,1:T(8,128)S(1)}, f32[512,1,5,128]{3,0,2,1:T(8,128)}) %get-tuple-element.1135, (pred[512,512]{0,1:T(8,128)(4,1)S(1)}, ...), branch_computations={%region_34.35_spmd, %region_35.0_spmd} | conditional | flops 688791040 | bytes 20217888 | solution.py:132
  124.3 3.9 %fusion.94 = f32[512,1,5,128]{3,0,2,1:T(8,128)} fusion(f32[512,512,5]{1,0,2:T(8,128)S(1)} %get-tuple-element.995, f32[512,5]{0,1:T(8,128)S(1)} %bitcast.1509, pred[512,512]{0,1:T(8,128)(4,1)S(1)} %get-tuple-element.301, f32[512,1,5,128]{3,0,2,1:T(8,128)} %get-tuple-element.305, f32[512,5]{0,1:T(8,128)S(1)} %get-tuple-element.976, ...), kind=kOutput, calls=%fused_computation.93 | convolution fusion | flops 342753280 | bytes 8278016 | tf_op jit(solution)/shard_map/cond/branch_1_fun/bkgt,tkd->bkgd/dot_general | solution.py:50
  129.5 6.2 %conditional.21 = ((f32[512,1,5]{0,2,1:T(8,128)S(1)}, f32[512,1,5]{0,2,1:T(8,128)S(1)}, f32[512,1,5,128]{3,0,2,1:T(8,128)})) conditional(s32[]{:T(128)} %convert_element_type.221, (f32[512,1,5]{0,2,1:T(8,128)S(1)}, f32[512,1,5]{0,2,1:T(8,128)S(1)}, f32[512,1,5,128]{3,0,2,1:T(8,128)}) %get-tuple-element.1136, (pred[512,512]{0,1:T(8,128)(4,1)S(1)}, ...), branch_computations={%region_39.40_spmd, %region_40.0_spmd} | conditional | flops 688791040 | bytes 20217888 | solution.py:132
  130.6 3.9 %fusion.115 = f32[512,1,5,128]{3,0,2,1:T(8,128)} fusion(f32[512,512,5]{1,0,2:T(8,128)S(1)} %get-tuple-element.997, f32[512,5]{0,1:T(8,128)S(1)} %bitcast.1511, pred[512,512]{0,1:T(8,128)(4,1)S(1)} %get-tuple-element.308, f32[512,1,5,128]{3,0,2,1:T(8,128)} %get-tuple-element.312, f32[512,5]{0,1:T(8,128)S(1)} %get-tuple-element.978, ...), kind=kOutput, calls=%fused_computation.114 | convolution fusion | flops 342753280 | bytes 8278016 | tf_op jit(solution)/shard_map/cond/branch_1_fun/bkgt,tkd->bkgd/dot_general | solution.py:50
  135.8 6.4 %conditional.22 = ((f32[512,1,5]{0,2,1:T(8,128)S(1)}, f32[512,1,5]{0,2,1:T(8,128)S(1)}, f32[512,1,5,128]{3,0,2,1:T(8,128)})) conditional(s32[]{:T(128)} %convert_element_type.219, (f32[512,1,5]{0,2,1:T(8,128)S(1)}, f32[512,1,5]{0,2,1:T(8,128)S(1)}, f32[512,1,5,128]{3,0,2,1:T(8,128)}) %get-tuple-element.1137, (pred[512,512]{0,1:T(8,128)(4,1)S(1)}, ...), branch_computations={%region_44.45_spmd, %region_45.48_spmd} | conditional | flops 688791040 | bytes 20217888 | solution.py:132
  137.1 3.9 %fusion.136 = f32[512,1,5,128]{3,0,2,1:T(8,128)} fusion(f32[512,512,5]{1,0,2:T(8,128)S(1)} %get-tuple-element.999, f32[512,5]{0,1:T(8,128)S(1)} %bitcast.1513, pred[512,512]{0,1:T(8,128)(4,1)S(1)} %get-tuple-element.315, f32[512,1,5,128]{3,0,2,1:T(8,128)} %get-tuple-element.319, f32[512,5]{0,1:T(8,128)S(1)} %get-tuple-element.980, ...), kind=kOutput, calls=%fused_computation.135 | convolution fusion | flops 342753280 | bytes 8278016 | tf_op jit(solution)/shard_map/cond/branch_1_fun/bkgt,tkd->bkgd/dot_general | solution.py:50
  142.3 8.0 %conditional.23 = (f32[512,1,5]{0,2,1:T(8,128)S(1)}, f32[512,1,5,128]{0,3,2,1:T(8,128)S(1)}, f32[512,1,5]{0,2,1:T(8,128)S(1)}) conditional(s32[]{:T(128)} %convert_element_type.217, (f32[512,1,5]{0,2,1:T(8,128)S(1)}, f32[512,1,5]{0,2,1:T(8,128)S(1)}, f32[512,1,5,128]{3,0,2,1:T(8,128)}) %get-tuple-element.1138, ...), branch_computations={%region_49.50_spmd.clone, %region_50.53_spmd.clone} | conditional | flops 688796160 | bytes 23353396 | solution.py:132
  143.4 3.9 %fusion.373 = f32[512,1,5,128]{3,0,2,1:T(8,128)} fusion(f32[512,512,5]{1,0,2:T(8,128)S(1)} %get-tuple-element.1003, f32[512,5]{0,1:T(8,128)S(1)} %get-tuple-element.1001, pred[512,512]{0,1:T(8,128)(4,1)S(1)} %get-tuple-element.940, f32[512,1,5,128]{3,0,2,1:T(8,128)} %get-tuple-element.945, f32[512,5]{0,1:T(8,128)S(1)} %get-tuple-element.1000, ...), kind=kOutput, calls=%fused_computation.397 | convolution fusion | flops 342753280 | bytes 8278016 | tf_op jit(solution)/shard_map/cond/branch_1_fun/bkgt,tkd->bkgd/dot_general | solution.py:50
  152.2 4.2 %all-to-all-start.3 = ((bf16[4,128,640]{1,2,0:T(8,128)(2,1)}), bf16[4,128,640]{1,2,0:T(8,128)(2,1)}, u32[]{:S(2)}, u32[]{:S(2)}) async-start(bf16[4,128,640]{1,2,0:T(8,128)(2,1)} %copy.237), calls=%async_computation.3 | async-start | bytes 1310720 | tf_op jit(solution)/shard_map/all_to_all | solution.py:174
  156.4 4.7 %fusion.392 = bf16[512,5,512]{0,2,1:T(8,128)(2,1)S(1)} fusion(f32[512,512,5]{1,0,2:T(8,128)} %copy-done.2, f32[512,5]{0,1:T(8,128)} %get-tuple-element.984, f32[512,5]{0,1:T(8,128)S(1)} %bitcast.1515, pred[512,512]{0,1:T(8,128)(4,1)} %get-tuple-element.1030, bf16[512,128,1]{1,0,2:T(8,128)(2,1)} %bitcast.1499, bf16[512,5,128]{0,2,1:T(8,128)(2,1)} %reshape.987), kind=kOutput, calls=%fused_computation.423 | convolution fusion | flops 344719360 | bytes 8933376 | tf_op jit(solution)/shard_map/cond/branch_1_fun/bkgd,tkd->bkgt/dot_general | solution.py:73
  162.8 7.4 %conditional.24 = (f32[512,1,5,128]{3,0,2,1:T(8,128)S(1)}, f32[2,512,128]{2,1,0:T(8,128)}) conditional(s32[]{:T(128)} %convert_element_type.231, () %tuple.130, (pred[512,512]{0,1:T(8,128)(4,1)S(1)}, bf16[512,1,128]{2,0,1:T(8,128)(2,1)S(1)}, bf16[512,1,5,128]{0,3,2,1:T(8,128)(2,1)S(1)}, f32[512,1,5]{0,2,1:T(8,128)S(1)}, ...), branch_computations={%region_54.55_spmd, %region_55.56_spmd} | conditional | flops 1693974528 | bytes 30046224 | solution.py:167
  172.2 8.1 %conditional.25 = (f32[512,1,5,128]{3,0,2,1:T(8,128)S(1)}, f32[2,512,128]{2,1,0:T(8,128)}) conditional(s32[]{:T(128)} %convert_element_type.229, () %tuple.132, (pred[512,512]{0,1:T(8,128)(4,1)}, bf16[512,1,128]{2,0,1:T(8,128)(2,1)}, bf16[512,1,5,128]{0,3,2,1:T(8,128)(2,1)S(1)}, f32[512,1,5]{0,2,1:T(8,128)S(1)}, bf16[512,1,128]{2,0,1:T(8,128)(2,1)}, ...), branch_computations={%region_56.57_spmd, %region_57.58_spmd} | conditional | flops 1693974528 | bytes 34805916 | solution.py:167
  182.3 7.5 %conditional.26 = (f32[512,1,5,128]{3,0,2,1:T(8,128)S(1)}, f32[2,512,128]{2,1,0:T(8,128)}) conditional(s32[]{:T(128)} %convert_element_type.227, () %tuple.134, (pred[512,512]{0,1:T(8,128)(4,1)}, bf16[512,1,128]{2,0,1:T(8,128)(2,1)S(1)}, bf16[512,1,5,128]{0,3,2,1:T(8,128)(2,1)S(1)}, f32[512,1,5]{0,2,1:T(8,128)S(1)}, ...), branch_computations={%region_58.59_spmd, %region_59.60_spmd} | conditional | flops 1693974528 | bytes 34281600 | solution.py:167
  191.9 8.1 %conditional.27 = (f32[512,1,5,128]{3,0,2,1:T(8,128)S(1)}, f32[2,512,128]{2,1,0:T(8,128)}) conditional(s32[]{:T(128)} %convert_element_type.225, () %tuple.136, (pred[512,512]{0,1:T(8,128)(4,1)}, bf16[512,1,128]{2,0,1:T(8,128)(2,1)}, bf16[512,1,5,128]{0,3,2,1:T(8,128)(2,1)S(1)}, f32[512,1,5]{0,2,1:T(8,128)S(1)}, bf16[512,1,128]{2,0,1:T(8,128)(2,1)}, ...), branch_computations={%region_60.61_spmd, %region_61.62_spmd} | conditional | flops 1693974528 | bytes 34805916 | solution.py:167
  201.9 7.6 %conditional.28 = (f32[512,1,5,128]{3,0,2,1:T(8,128)S(1)}, f32[2,512,128]{2,1,0:T(8,128)}) conditional(s32[]{:T(128)} %convert_element_type.223, () %tuple.138, (pred[512,512]{0,1:T(8,128)(4,1)}, bf16[512,1,128]{2,0,1:T(8,128)(2,1)S(1)}, bf16[512,1,5,128]{0,3,2,1:T(8,128)(2,1)S(1)}, f32[512,1,5]{0,2,1:T(8,128)S(1)}, ...), branch_computations={%region_62.63_spmd, %region_63.64_spmd} | conditional | flops 1693974528 | bytes 34281600 | solution.py:167
  211.6 8.1 %conditional.29 = (f32[512,1,5,128]{3,0,2,1:T(8,128)S(1)}, f32[2,512,128]{2,1,0:T(8,128)}) conditional(s32[]{:T(128)} %convert_element_type.221, () %tuple.140, (pred[512,512]{0,1:T(8,128)(4,1)}, bf16[512,1,128]{2,0,1:T(8,128)(2,1)}, bf16[512,1,5,128]{0,3,2,1:T(8,128)(2,1)S(1)}, f32[512,1,5]{0,2,1:T(8,128)S(1)}, bf16[512,1,128]{2,0,1:T(8,128)(2,1)}, ...), branch_computations={%region_64.65_spmd, %region_65.66_spmd} | conditional | flops 1693974528 | bytes 34805916 | solution.py:167
  220.8 7.7 %conditional.30 = (f32[512,1,5,128]{3,0,2,1:T(8,128)S(1)}, f32[2,512,128]{2,1,0:T(8,128)}) conditional(s32[]{:T(128)} %convert_element_type.219, () %tuple.142, (pred[512,512]{0,1:T(8,128)(4,1)}, bf16[512,1,128]{2,0,1:T(8,128)(2,1)S(1)}, bf16[512,1,5,128]{0,3,2,1:T(8,128)(2,1)S(1)}, f32[512,1,5]{0,2,1:T(8,128)S(1)}, ...), branch_computations={%region_66.67_spmd, %region_67.68_spmd} | conditional | flops 1693974528 | bytes 34281600 | solution.py:167
  229.6 7.8 %conditional.31 = (f32[512,1,5,128]{3,0,2,1:T(8,128)}, f32[2,512,128]{2,1,0:T(8,128)S(1)}) conditional(s32[]{:T(128)} %convert_element_type.217, () %tuple.144, (pred[512,512]{0,1:T(8,128)(4,1)}, bf16[512,1,128]{2,0,1:T(8,128)(2,1)S(1)}, bf16[512,1,5,128]{0,3,2,1:T(8,128)(2,1)S(1)}, f32[512,1,5]{0,2,1:T(8,128)S(1)}, ...), branch_computations={%region_68.69_spmd, %region_69.70_spmd} | conditional | flops 1693974528 | bytes 34281600 | solution.py:167
  238.2 4.3 %add_convert_fusion = bf16[512,1,5,128]{3,0,2,1:T(8,128)(2,1)S(1)} fusion(f32[512,1,5,128]{3,0,2,1:T(8,128)} %get-tuple-element.459, f32[512,1,5,128]{3,0,2,1:T(8,128)} %copy-done.8, f32[512,1,5,128]{3,0,2,1:T(8,128)} %copy-done.7, f32[512,1,5,128]{3,0,2,1:T(8,128)} %copy-done.6, f32[512,1,5,128]{3,0,2,1:T(8,128)} %copy-done.5, ...), kind=kLoop, calls=%fused_computation.433 | loop fusion | flops 2949120 | bytes 12451840 | tf_op jit(solution)/shard_map/convert_element_type | solution.py:178
  243.9 3.4 %fusion.410 = f32[1,512,128]{2,1,0:T(8,128)} fusion(bf16[512,5,512]{0,2,1:T(8,128)(2,1)} %copy-done.10, bf16[512,5,128]{0,2,1:T(8,128)(2,1)} %copy-done.9), kind=kOutput, calls=%fused_computation.438 | convolution fusion | flops 335609856 | bytes 3538944 | tf_op jit(solution)/shard_map/cond/branch_1_fun/bkgt,bkgd->tkd/dot_general | solution.py:82
  253.1 4.7 %fusion.411 = f32[1,512,128]{2,1,0:T(8,128)} fusion(bf16[512,5,128]{0,2,1:T(8,128)(2,1)S(1)} %copy-done.55, f32[512,512,5]{1,0,2:T(8,128)} %copy-done.2, f32[512,5]{0,1:T(8,128)S(1)} %bitcast.1516, pred[512,512]{0,1:T(8,128)(4,1)S(1)} %copy-done.26), kind=kOutput, calls=%fused_computation.439 | convolution fusion | flops 342097920 | bytes 6432768 | tf_op jit(solution)/shard_map/cond/branch_1_fun/bkgt,bkgd->tkd/dot_general | solution.py:67
  257.8 4.7 %all-to-all-start.5 = ((bf16[4,128,640]{1,2,0:T(8,128)(2,1)}), bf16[4,128,640]{1,2,0:T(8,128)(2,1)S(1)}, u32[]{:S(2)}, u32[]{:S(2)}) async-start(bf16[4,128,640]{1,2,0:T(8,128)(2,1)} %copy.260), calls=%async_computation.5 | async-start | bytes 1310720 | tf_op jit(solution)/shard_map/all_to_all | solution.py:177
  264.0 4.2 %collective-permute-done.14 = f32[2,512,128]{2,1,0:T(8,128)S(1)} collective-permute-done((f32[2,512,128]{2,1,0:T(8,128)}, f32[2,512,128]{2,1,0:T(8,128)S(1)}, u32[]{:S(2)}, u32[]{:S(2)}) %collective-permute-start.14) | collective-permute-done | bytes 524320 | tf_op jit(solution)/shard_map/ppermute | solution.py:17
  268.2 5.6 %collective-permute-done.15 = f32[2,512,128]{2,1,0:T(8,128)S(1)} collective-permute-done((f32[2,512,128]{2,1,0:T(8,128)}, f32[2,512,128]{2,1,0:T(8,128)S(1)}, u32[]{:S(2)}, u32[]{:S(2)}) %collective-permute-start.15) | collective-permute-done | bytes 524320 | tf_op jit(solution)/shard_map/ppermute | solution.py:17
  276.5 4.7 %all-to-all-start.6 = ((bf16[4,128,128]{2,1,0:T(8,128)(2,1)}), bf16[4,128,128]{2,1,0:T(8,128)(2,1)S(1)}, u32[]{:S(2)}, u32[]{:S(2)}) async-start(bf16[4,128,128]{2,1,0:T(8,128)(2,1)} %bitcast.402), calls=%async_computation.6 | async-start | bytes 262144 | tf_op jit(solution)/shard_map/all_to_all | solution.py:184
  287.3 3.3 %all-to-all-start.7 = ((bf16[4,128,128]{2,1,0:T(8,128)(2,1)}), bf16[4,128,128]{2,1,0:T(8,128)(2,1)S(1)}, u32[]{:S(2)}, u32[]{:S(2)}) async-start(bf16[4,128,128]{2,1,0:T(8,128)(2,1)} %bitcast.404), calls=%async_computation.7 | async-start | bytes 262144 | tf_op jit(solution)/shard_map/all_to_all | solution.py:187
  291.3 5.3 %all-to-all-done.7 = bf16[4,128,128]{2,1,0:T(8,128)(2,1)S(1)} async-done(((bf16[4,128,128]{2,1,0:T(8,128)(2,1)}), bf16[4,128,128]{2,1,0:T(8,128)(2,1)S(1)}, u32[]{:S(2)}, u32[]{:S(2)}) %all-to-all-start.7) | async-done | bytes 131104 | tf_op jit(solution)/shard_map/all_to_all | solution.py:187
  (334 shorter events, 148.1 us)
Async XLA Ops:
  1.5 46.2 %copy-start.54 = (bf16[128,2560]{1,0:T(8,128)(2,1)S(1)}, bf16[128,2560]{1,0:T(8,128)(2,1)}, u32[]{:S(2)}) copy-start(bf16[128,2560]{1,0:T(8,128)(2,1)} %param.40) | copy-start | bytes 1966084
  2.2 13.2 %all-to-all-start = ((bf16[128,4,128]{2,0,1:T(8,128)(2,1)}), bf16[128,4,128]{2,0,1:T(8,128)(2,1)S(1)}, u32[]{:S(2)}, u32[]{:S(2)}) async-start(bf16[128,4,128]{2,0,1:T(8,128)(2,1)} %copy_bitcast_fusion.3), calls=%async_computation | async-start | bytes 262144 | tf_op jit(solution)/shard_map/all_to_all | solution.py:93
  15.4 75.7 %copy-start.52 = (bf16[128,4,128]{2,0,1:T(8,128)(2,1)}, bf16[128,4,128]{2,0,1:T(8,128)(2,1)S(1)}, u32[]{:S(2)}) copy-start(bf16[128,4,128]{2,0,1:T(8,128)(2,1)S(1)} %all-to-all-done) | copy-start | bytes 393220
  15.4 10.8 %all-to-all-start.2 = ((bf16[128,4,128]{2,0,1:T(8,128)(2,1)}), bf16[128,4,128]{2,0,1:T(8,128)(2,1)S(1)}, u32[]{:S(2)}, u32[]{:S(2)}) async-start(bf16[128,4,128]{2,0,1:T(8,128)(2,1)} %copy_bitcast_fusion.2), calls=%async_computation.2 | async-start | bytes 262144 | tf_op jit(solution)/shard_map/all_to_all | solution.py:94
  26.2 61.9 %copy-start.57 = (bf16[128,4,128]{2,0,1:T(8,128)(2,1)}, bf16[128,4,128]{2,0,1:T(8,128)(2,1)S(1)}, u32[]{:S(2)}) copy-start(bf16[128,4,128]{2,0,1:T(8,128)(2,1)S(1)} %all-to-all-done.2) | copy-start | bytes 393220
  26.2 47.4 %all-to-all-start.1 = ((bf16[128,4,640]{0,2,1:T(8,128)(2,1)}), bf16[128,4,640]{0,2,1:T(8,128)(2,1)S(1)}, u32[]{:S(2)}, u32[]{:S(2)}) async-start(bf16[128,4,640]{0,2,1:T(8,128)(2,1)} %bitcast.341), calls=%async_computation.1 | async-start | bytes 1310720 | tf_op jit(solution)/shard_map/all_to_all | solution.py:92
  29.8 27.7 %collective-permute-start.7 = (bf16[2,512,128]{2,1,0:T(8,128)(2,1)S(1)}, bf16[2,512,128]{2,1,0:T(8,128)(2,1)S(1)}, u32[]{:S(2)}, u32[]{:S(2)}) collective-permute-start(bf16[2,512,128]{2,1,0:T(8,128)(2,1)S(1)} %pad_maximum_fusion.8), channel_id=1, source_target_pairs={{0,32},{4,36},{8,40},{12,44},{16,48},{20,52},{24,56},{28,60},{32,6... | collective-permute-start | bytes 786440 | tf_op jit(solution)/shard_map/ppermute | solution.py:17
  34.2 63.1 %copy-start.23 = (pred[512,512]{0,1:T(8,128)(4,1)}, pred[512,512]{0,1:T(8,128)(4,1)S(1)}, u32[]{:S(2)}) copy-start(pred[512,512]{0,1:T(8,128)(4,1)S(1)} %get-tuple-element.1033) | copy-start | bytes 786436
  34.2 95.3 %copy-start.21 = (pred[512,512]{0,1:T(8,128)(4,1)}, pred[512,512]{0,1:T(8,128)(4,1)S(1)}, u32[]{:S(2)}) copy-start(pred[512,512]{0,1:T(8,128)(4,1)S(1)} %get-tuple-element.1032) | copy-start | bytes 786436
  34.2 101.5 %copy-start.19 = (pred[512,512]{0,1:T(8,128)(4,1)}, pred[512,512]{0,1:T(8,128)(4,1)S(1)}, u32[]{:S(2)}) copy-start(pred[512,512]{0,1:T(8,128)(4,1)S(1)} %get-tuple-element.1031) | copy-start | bytes 786436
  34.2 25.9 %collective-permute-start.6 = (bf16[2,512,128]{2,1,0:T(8,128)(2,1)S(1)}, bf16[2,512,128]{2,1,0:T(8,128)(2,1)S(1)}, u32[]{:S(2)}, u32[]{:S(2)}) collective-permute-start(bf16[2,512,128]{2,1,0:T(8,128)(2,1)S(1)} %pad_maximum_fusion.8), channel_id=1, source_target_pairs={{0,28},{4,32},{8,36},{12,40},{16,44},{20,48},{24,52},{28,56},{32,6... | collective-permute-start | bytes 786440 | tf_op jit(solution)/shard_map/ppermute | solution.py:17
  48.8 14.7 %collective-permute-start.5 = (bf16[2,512,128]{2,1,0:T(8,128)(2,1)S(1)}, bf16[2,512,128]{2,1,0:T(8,128)(2,1)S(1)}, u32[]{:S(2)}, u32[]{:S(2)}) collective-permute-start(bf16[2,512,128]{2,1,0:T(8,128)(2,1)S(1)} %pad_maximum_fusion.8), channel_id=1, source_target_pairs={{0,24},{4,28},{8,32},{12,36},{16,40},{20,44},{24,48},{28,52},{32,5... | collective-permute-start | bytes 786440 | tf_op jit(solution)/shard_map/ppermute | solution.py:17
  53.6 13.6 %collective-permute-start.4 = (bf16[2,512,128]{2,1,0:T(8,128)(2,1)S(1)}, bf16[2,512,128]{2,1,0:T(8,128)(2,1)S(1)}, u32[]{:S(2)}, u32[]{:S(2)}) collective-permute-start(bf16[2,512,128]{2,1,0:T(8,128)(2,1)S(1)} %pad_maximum_fusion.8), channel_id=1, source_target_pairs={{0,20},{4,24},{8,28},{12,32},{16,36},{20,40},{24,44},{28,48},{32,5... | collective-permute-start | bytes 786440 | tf_op jit(solution)/shard_map/ppermute | solution.py:17
  55.5 17.4 %collective-permute-start.3 = (bf16[2,512,128]{2,1,0:T(8,128)(2,1)S(1)}, bf16[2,512,128]{2,1,0:T(8,128)(2,1)S(1)}, u32[]{:S(2)}, u32[]{:S(2)}) collective-permute-start(bf16[2,512,128]{2,1,0:T(8,128)(2,1)S(1)} %pad_maximum_fusion.8), channel_id=1, source_target_pairs={{0,16},{4,20},{8,24},{12,28},{16,32},{20,36},{24,40},{28,44},{32,4... | collective-permute-start | bytes 786440 | tf_op jit(solution)/shard_map/ppermute | solution.py:17
  57.5 20.9 %collective-permute-start.2 = (bf16[2,512,128]{2,1,0:T(8,128)(2,1)S(1)}, bf16[2,512,128]{2,1,0:T(8,128)(2,1)S(1)}, u32[]{:S(2)}, u32[]{:S(2)}) collective-permute-start(bf16[2,512,128]{2,1,0:T(8,128)(2,1)S(1)} %pad_maximum_fusion.8), channel_id=1, source_target_pairs={{0,12},{4,16},{8,20},{12,24},{16,28},{20,32},{24,36},{28,40},{32,4... | collective-permute-start | bytes 786440 | tf_op jit(solution)/shard_map/ppermute | solution.py:17
  60.1 24.3 %collective-permute-start.1 = (bf16[2,512,128]{2,1,0:T(8,128)(2,1)S(1)}, bf16[2,512,128]{2,1,0:T(8,128)(2,1)S(1)}, u32[]{:S(2)}, u32[]{:S(2)}) collective-permute-start(bf16[2,512,128]{2,1,0:T(8,128)(2,1)S(1)} %pad_maximum_fusion.8), channel_id=1, source_target_pairs={{0,8},{4,12},{8,16},{12,20},{16,24},{20,28},{24,32},{28,36},{32,40... | collective-permute-start | bytes 786440 | tf_op jit(solution)/shard_map/ppermute | solution.py:17
  63.6 23.3 %collective-permute-start = (bf16[2,512,128]{2,1,0:T(8,128)(2,1)S(1)}, bf16[2,512,128]{2,1,0:T(8,128)(2,1)S(1)}, u32[]{:S(2)}, u32[]{:S(2)}) collective-permute-start(bf16[2,512,128]{2,1,0:T(8,128)(2,1)S(1)} %pad_maximum_fusion.8), channel_id=1, source_target_pairs={{0,4},{4,8},{8,12},{12,16},{16,20},{20,24},{24,28},{28,32},{32,36}... | collective-permute-start | bytes 786440 | tf_op jit(solution)/shard_map/ppermute | solution.py:17
  73.6 15.6 %all-to-all-start.4 = ((bf16[128,4,640]{0,2,1:T(8,128)(2,1)}), bf16[128,4,640]{0,2,1:T(8,128)(2,1)S(1)}, u32[]{:S(2)}, u32[]{:S(2)}) async-start(bf16[128,4,640]{0,2,1:T(8,128)(2,1)} %bitcast.378), calls=%async_computation.4 | async-start | bytes 1310720 | tf_op jit(solution)/shard_map/all_to_all | solution.py:95
  90.0 72.1 %copy-start.11 = (bf16[512,1,5,128]{0,3,2,1:T(8,128)(2,1)}, bf16[512,1,5,128]{0,3,2,1:T(8,128)(2,1)S(1)}, u32[]{:S(2)}) copy-start(bf16[512,1,5,128]{0,3,2,1:T(8,128)(2,1)S(1)} %reshape.988) | copy-start | bytes 1966084
  97.4 6.8 %copy-start.35 = (pred[512,512]{0,1:T(8,128)(4,1)S(1)}, pred[512,512]{0,1:T(8,128)(4,1)}, u32[]{:S(2)}) copy-start(pred[512,512]{0,1:T(8,128)(4,1)} %get-tuple-element.1026) | copy-start | bytes 786436
  97.4 6.8 %copy-start.48 = (bf16[512,1,128]{2,0,1:T(8,128)(2,1)S(1)}, bf16[512,1,128]{2,0,1:T(8,128)(2,1)}, u32[]{:S(2)}) copy-start(bf16[512,1,128]{2,0,1:T(8,128)(2,1)} %get-tuple-element.1019) | copy-start | bytes 393220
  97.4 6.8 %copy-start.71 = (bf16[512,1,128]{2,0,1:T(8,128)(2,1)S(1)}, bf16[512,1,128]{2,0,1:T(8,128)(2,1)}, u32[]{:S(2)}) copy-start(bf16[512,1,128]{2,0,1:T(8,128)(2,1)} %get-tuple-element.1018) | copy-start | bytes 393220
  104.2 6.3 %copy-start.33 = (pred[512,512]{0,1:T(8,128)(4,1)S(1)}, pred[512,512]{0,1:T(8,128)(4,1)}, u32[]{:S(2)}) copy-start(pred[512,512]{0,1:T(8,128)(4,1)} %get-tuple-element.1027) | copy-start | bytes 786436
  104.2 6.3 %copy-start.46 = (bf16[512,1,128]{2,0,1:T(8,128)(2,1)S(1)}, bf16[512,1,128]{2,0,1:T(8,128)(2,1)}, u32[]{:S(2)}) copy-start(bf16[512,1,128]{2,0,1:T(8,128)(2,1)} %get-tuple-element.1017) | copy-start | bytes 393220
  104.2 6.3 %copy-start.69 = (bf16[512,1,128]{2,0,1:T(8,128)(2,1)S(1)}, bf16[512,1,128]{2,0,1:T(8,128)(2,1)}, u32[]{:S(2)}) copy-start(bf16[512,1,128]{2,0,1:T(8,128)(2,1)} %get-tuple-element.1016) | copy-start | bytes 393220
  110.5 6.3 %copy-start.31 = (pred[512,512]{0,1:T(8,128)(4,1)S(1)}, pred[512,512]{0,1:T(8,128)(4,1)}, u32[]{:S(2)}) copy-start(pred[512,512]{0,1:T(8,128)(4,1)} %get-tuple-element.1028) | copy-start | bytes 786436
  116.8 6.4 %copy-start.29 = (pred[512,512]{0,1:T(8,128)(4,1)S(1)}, pred[512,512]{0,1:T(8,128)(4,1)}, u32[]{:S(2)}) copy-start(pred[512,512]{0,1:T(8,128)(4,1)} %get-tuple-element.1029) | copy-start | bytes 786436
  116.8 6.4 %copy-start.42 = (bf16[512,1,128]{2,0,1:T(8,128)(2,1)S(1)}, bf16[512,1,128]{2,0,1:T(8,128)(2,1)}, u32[]{:S(2)}) copy-start(bf16[512,1,128]{2,0,1:T(8,128)(2,1)} %get-tuple-element.1013) | copy-start | bytes 393220
  116.8 6.4 %copy-start.65 = (bf16[512,1,128]{2,0,1:T(8,128)(2,1)S(1)}, bf16[512,1,128]{2,0,1:T(8,128)(2,1)}, u32[]{:S(2)}) copy-start(bf16[512,1,128]{2,0,1:T(8,128)(2,1)} %get-tuple-element.1012) | copy-start | bytes 393220
  135.8 6.5 %copy-start.27 = (pred[512,512]{0,1:T(8,128)(4,1)S(1)}, pred[512,512]{0,1:T(8,128)(4,1)}, u32[]{:S(2)}) copy-start(pred[512,512]{0,1:T(8,128)(4,1)} %get-tuple-element.1025) | copy-start | bytes 786436
  135.8 6.5 %copy-start.37 = (bf16[512,1,128]{2,0,1:T(8,128)(2,1)S(1)}, bf16[512,1,128]{2,0,1:T(8,128)(2,1)}, u32[]{:S(2)}) copy-start(bf16[512,1,128]{2,0,1:T(8,128)(2,1)} %get-tuple-element.1007) | copy-start | bytes 393220
  152.2 105.6 %all-to-all-start.3 = ((bf16[4,128,640]{1,2,0:T(8,128)(2,1)}), bf16[4,128,640]{1,2,0:T(8,128)(2,1)}, u32[]{:S(2)}, u32[]{:S(2)}) async-start(bf16[4,128,640]{1,2,0:T(8,128)(2,1)} %copy.237), calls=%async_computation.3 | async-start | bytes 1310720 | tf_op jit(solution)/shard_map/all_to_all | solution.py:174
  170.2 10.2 %copy-start.47 = (bf16[512,1,128]{2,0,1:T(8,128)(2,1)S(1)}, bf16[512,1,128]{2,0,1:T(8,128)(2,1)}, u32[]{:S(2)}) copy-start(bf16[512,1,128]{2,0,1:T(8,128)(2,1)} %get-tuple-element.1017) | copy-start | bytes 393220
  170.2 77.1 %collective-permute-start.8 = (f32[2,512,128]{2,1,0:T(8,128)}, f32[2,512,128]{2,1,0:T(8,128)}, u32[]{:S(2)}, u32[]{:S(2)}) collective-permute-start(f32[2,512,128]{2,1,0:T(8,128)} %get-tuple-element.460), channel_id=1, source_target_pairs={{4,0},{8,4},{12,8},{16,12},{20,16},{24,20},{28,24},{32,28},{36,32}... | collective-permute-start | bytes 1572872 | tf_op jit(solution)/shard_map/ppermute | solution.py:17
  180.3 68.9 %collective-permute-start.9 = (f32[2,512,128]{2,1,0:T(8,128)}, f32[2,512,128]{2,1,0:T(8,128)}, u32[]{:S(2)}, u32[]{:S(2)}) collective-permute-start(f32[2,512,128]{2,1,0:T(8,128)} %get-tuple-element.461), channel_id=1, source_target_pairs={{8,0},{12,4},{16,8},{20,12},{24,16},{28,20},{32,24},{36,28},{40,32... | collective-permute-start | bytes 1572872 | tf_op jit(solution)/shard_map/ppermute | solution.py:17
  189.8 10.2 %copy-start.43 = (bf16[512,1,128]{2,0,1:T(8,128)(2,1)S(1)}, bf16[512,1,128]{2,0,1:T(8,128)(2,1)}, u32[]{:S(2)}) copy-start(bf16[512,1,128]{2,0,1:T(8,128)(2,1)} %get-tuple-element.1013) | copy-start | bytes 393220
  189.8 61.4 %collective-permute-start.10 = (f32[2,512,128]{2,1,0:T(8,128)}, f32[2,512,128]{2,1,0:T(8,128)}, u32[]{:S(2)}, u32[]{:S(2)}) collective-permute-start(f32[2,512,128]{2,1,0:T(8,128)} %get-tuple-element.462), channel_id=1, source_target_pairs={{12,0},{16,4},{20,8},{24,12},{28,16},{32,20},{36,24},{40,28},{44,3... | collective-permute-start | bytes 1572872 | tf_op jit(solution)/shard_map/ppermute | solution.py:17
  200.0 62.5 %collective-permute-start.11 = (f32[2,512,128]{2,1,0:T(8,128)}, f32[2,512,128]{2,1,0:T(8,128)}, u32[]{:S(2)}, u32[]{:S(2)}) collective-permute-start(f32[2,512,128]{2,1,0:T(8,128)} %get-tuple-element.463), channel_id=1, source_target_pairs={{16,0},{20,4},{24,8},{28,12},{32,16},{36,20},{40,24},{44,28},{48,3... | collective-permute-start | bytes 1572872 | tf_op jit(solution)/shard_map/ppermute | solution.py:17
  209.6 53.0 %collective-permute-start.12 = (f32[2,512,128]{2,1,0:T(8,128)}, f32[2,512,128]{2,1,0:T(8,128)}, u32[]{:S(2)}, u32[]{:S(2)}) collective-permute-start(f32[2,512,128]{2,1,0:T(8,128)} %get-tuple-element.464), channel_id=1, source_target_pairs={{20,0},{24,4},{28,8},{32,12},{36,16},{40,20},{44,24},{48,28},{52,3... | collective-permute-start | bytes 1572872 | tf_op jit(solution)/shard_map/ppermute | solution.py:17
  242.5 10.6 %copy-start.26 = (pred[512,512]{0,1:T(8,128)(4,1)S(1)}, pred[512,512]{0,1:T(8,128)(4,1)}, u32[]{:S(2)}) copy-start(pred[512,512]{0,1:T(8,128)(4,1)} %get-tuple-element.1030) | copy-start | bytes 786436
  242.5 10.6 %copy-start.55 = (bf16[512,5,128]{0,2,1:T(8,128)(2,1)S(1)}, bf16[512,5,128]{0,2,1:T(8,128)(2,1)}, u32[]{:S(2)}) copy-start(bf16[512,5,128]{0,2,1:T(8,128)(2,1)} %reshape.987) | copy-start | bytes 1966084
  247.3 16.7 %collective-permute-start.13 = (f32[2,512,128]{2,1,0:T(8,128)}, f32[2,512,128]{2,1,0:T(8,128)S(1)}, u32[]{:S(2)}, u32[]{:S(2)}) collective-permute-start(f32[2,512,128]{2,1,0:T(8,128)} %get-tuple-element.465), channel_id=1, source_target_pairs={{24,0},{28,4},{32,8},{36,12},{40,16},{44,20},{48,24},{52,28},{56,3... | collective-permute-start | bytes 1572872 | tf_op jit(solution)/shard_map/ppermute | solution.py:17
  249.2 18.9 %collective-permute-start.14 = (f32[2,512,128]{2,1,0:T(8,128)}, f32[2,512,128]{2,1,0:T(8,128)S(1)}, u32[]{:S(2)}, u32[]{:S(2)}) collective-permute-start(f32[2,512,128]{2,1,0:T(8,128)} %get-tuple-element.466), channel_id=1, source_target_pairs={{28,0},{32,4},{36,8},{40,12},{44,16},{48,20},{52,24},{56,28},{60,3... | collective-permute-start | bytes 1572872 | tf_op jit(solution)/shard_map/ppermute | solution.py:17
  251.2 22.6 %collective-permute-start.15 = (f32[2,512,128]{2,1,0:T(8,128)}, f32[2,512,128]{2,1,0:T(8,128)S(1)}, u32[]{:S(2)}, u32[]{:S(2)}) collective-permute-start(f32[2,512,128]{2,1,0:T(8,128)} %copy-done.56), channel_id=1, source_target_pairs={{32,0},{36,4},{40,8},{44,12},{48,16},{52,20},{56,24},{60,28},{64,3... | collective-permute-start | bytes 1572872 | tf_op jit(solution)/shard_map/ppermute | solution.py:17
  253.1 44.1 %copy-start.1 = (bf16[128,512]{1,0:T(8,128)(2,1)S(1)}, bf16[128,512]{1,0:T(8,128)(2,1)}, u32[]{:S(2)}) copy-start(bf16[128,512]{1,0:T(8,128)(2,1)} %param.38) | copy-start | bytes 393220
  257.8 18.7 %all-to-all-start.5 = ((bf16[4,128,640]{1,2,0:T(8,128)(2,1)}), bf16[4,128,640]{1,2,0:T(8,128)(2,1)S(1)}, u32[]{:S(2)}, u32[]{:S(2)}) async-start(bf16[4,128,640]{1,2,0:T(8,128)(2,1)} %copy.260), calls=%async_computation.5 | async-start | bytes 1310720 | tf_op jit(solution)/shard_map/all_to_all | solution.py:177
  276.5 10.7 %all-to-all-start.6 = ((bf16[4,128,128]{2,1,0:T(8,128)(2,1)}), bf16[4,128,128]{2,1,0:T(8,128)(2,1)S(1)}, u32[]{:S(2)}, u32[]{:S(2)}) async-start(bf16[4,128,128]{2,1,0:T(8,128)(2,1)} %bitcast.402), calls=%async_computation.6 | async-start | bytes 262144 | tf_op jit(solution)/shard_map/all_to_all | solution.py:184
  287.3 9.3 %all-to-all-start.7 = ((bf16[4,128,128]{2,1,0:T(8,128)(2,1)}), bf16[4,128,128]{2,1,0:T(8,128)(2,1)S(1)}, u32[]{:S(2)}, u32[]{:S(2)}) async-start(bf16[4,128,128]{2,1,0:T(8,128)(2,1)} %bitcast.404), calls=%async_computation.7 | async-start | bytes 262144 | tf_op jit(solution)/shard_map/all_to_all | solution.py:187
  (59 other events, 149.8 us)

commit v2 on v1

v2 whole, which is shorter than its diff:
```python
import functools

import jax
import jax.numpy as jnp
from jax import lax
from jax.experimental import pallas as pl
from jax.experimental.pallas import tpu as pltpu
from jax.sharding import PartitionSpec as P

HD = 128
QH = 20
KVH = 4
LONG = 4096

NT = (((1,), (1,)), ((), ()))
TN = (((0,), (0,)), ((), ()))


def shifted(value, axis, by):
    peers = lax.axis_size(axis)
    pairs = [(i, i + by) for i in range(peers) if 0 <= i + by < peers]
    return lax.ppermute(value, axis, pairs)


def segment_of(position, doc_ends):
    return jnp.sum((position >= doc_ends).astype(jnp.int32))


def segments(first_row, row_count, doc_ends):
    position = first_row + jnp.arange(row_count, dtype=jnp.int32)
    return jnp.sum((position[:, None] >= doc_ends[None, :]).astype(jnp.int32), axis=1)


def block_visible(qseg_ref, kseg_ref, diagonal):
    visible = qseg_ref[...] == kseg_ref[...]
    if diagonal:
        rows = lax.broadcasted_iota(jnp.int32, visible.shape, 0)
        cols = lax.broadcasted_iota(jnp.int32, visible.shape, 1)
        visible = visible & (cols <= rows)
    return visible


def forward_kernel(live_ref, q_ref, k_ref, v_ref, qseg_ref, kseg_ref, m_in, l_in, acc_in,
                   m_out, l_out, acc_out, *, diagonal, scaling):
    @pl.when(live_ref[0] != 0)
    def _():
        scores = lax.dot_general(q_ref[...], k_ref[...], NT, preferred_element_type=jnp.float32)
        scores = scores * scaling
        visible = block_visible(qseg_ref, kseg_ref, diagonal)
        scores = jnp.where(visible, scores, -1e30)
        running = m_in[0][:, :1]
        newest = jnp.maximum(running, jnp.max(scores, axis=1, keepdims=True))
        weight = jnp.where(visible, jnp.exp(scores - newest), 0.0)
        shrink = jnp.exp(running - newest)
        denominator = l_in[0][:, :1] * shrink + jnp.sum(weight, axis=1, keepdims=True)
        mixed = jnp.dot(weight.astype(jnp.bfloat16), v_ref[...], preferred_element_type=jnp.float32)
        acc_out[...] = acc_in[...] * shrink + mixed
        m_out[0] = jnp.broadcast_to(newest, m_out.shape[1:])
        l_out[0] = jnp.broadcast_to(denominator, l_out.shape[1:])

    @pl.when(live_ref[0] == 0)
    def _():
        acc_out[...] = acc_in[...]
        m_out[...] = m_in[...]
        l_out[...] = l_in[...]


def backward_kernel(live_ref, q_ref, g_ref, lse_ref, dot_ref, k_ref, v_ref, qseg_ref, kseg_ref,
                    dq_in, dq_out, dk_out, dv_out, *, diagonal, scaling):
    head = pl.program_id(0)

    @pl.when(head == 0)
    def _():
        dk_out[...] = jnp.zeros_like(dk_out)
        dv_out[...] = jnp.zeros_like(dv_out)

    @pl.when(live_ref[0] != 0)
    def _():
        q = q_ref[...]
        g = g_ref[...]
        k = k_ref[...]
        scores = lax.dot_general(q, k, NT, preferred_element_type=jnp.float32) * scaling
        visible = block_visible(qseg_ref, kseg_ref, diagonal)
        scores = jnp.where(visible, scores, -1e30)
        probability = jnp.where(visible, jnp.exp(scores - lse_ref[0][:, :1]), 0.0)
        dv_out[...] += lax.dot_general(
            probability.astype(jnp.bfloat16), g, TN, preferred_element_type=jnp.float32
        )
        grad_prob = lax.dot_general(g, v_ref[...], NT, preferred_element_type=jnp.float32)
        grad_score = (probability * (grad_prob - dot_ref[0][:, :1])).astype(jnp.bfloat16)
        dq_out[...] = dq_in[...] + jnp.dot(grad_score, k, preferred_element_type=jnp.float32) * scaling
        dk_out[...] += lax.dot_general(grad_score, q, TN, preferred_element_type=jnp.float32) * scaling

    @pl.when(live_ref[0] == 0)
    def _():
        dq_out[...] = dq_in[...]


def forward_block(live, query, key, value, qseg, kseg, state, diagonal, scaling):
    length, width = query.shape
    heads = width // HD
    m, l, acc = state
    row_block = pl.BlockSpec((length, HD), lambda h, lv: (0, h))
    whole = pl.BlockSpec((length, HD), lambda h, lv: (0, 0))
    stat = pl.BlockSpec((1, length, HD), lambda h, lv: (h, 0, 0))
    grid_spec = pltpu.PrefetchScalarGridSpec(
        num_scalar_prefetch=1,
        grid=(heads,),
        in_specs=[
            row_block,
            whole,
            whole,
            pl.BlockSpec((length, 1), lambda h, lv: (0, 0)),
            pl.BlockSpec((1, length), lambda h, lv: (0, 0)),
            stat,
            stat,
            row_block,
        ],
        out_specs=[stat, stat, row_block],
    )
    return pl.pallas_call(
        functools.partial(forward_kernel, diagonal=diagonal, scaling=scaling),
        out_shape=(
            jax.ShapeDtypeStruct(m.shape, jnp.float32),
            jax.ShapeDtypeStruct(l.shape, jnp.float32),
            jax.ShapeDtypeStruct(acc.shape, jnp.float32),
        ),
        grid_spec=grid_spec,
        input_output_aliases={6: 0, 7: 1, 8: 2},
        cost_estimate=pl.CostEstimate(
            flops=4 * length * length * width,
            transcendentals=length * length * heads,
            bytes_accessed=40 * length * width,
        ),
        compiler_params=pltpu.CompilerParams(dimension_semantics=("arbitrary",)),
    )(live, query, key, value, qseg, kseg, m, l, acc)


def backward_block(live, query, grad, lse, rdot, key, value, qseg, kseg, dq, diagonal, scaling):
    length, width = query.shape
    heads = width // HD
    row_block = pl.BlockSpec((length, HD), lambda h, lv: (0, h))
    whole = pl.BlockSpec((length, HD), lambda h, lv: (0, 0))
    stat = pl.BlockSpec((1, length, HD), lambda h, lv: (h, 0, 0))
    grid_spec = pltpu.PrefetchScalarGridSpec(
        num_scalar_prefetch=1,
        grid=(heads,),
        in_specs=[
            row_block,
            row_block,
            stat,
            stat,
            whole,
            whole,
            pl.BlockSpec((length, 1), lambda h, lv: (0, 0)),
            pl.BlockSpec((1, length), lambda h, lv: (0, 0)),
            row_block,
        ],
        out_specs=[row_block, whole, whole],
    )
    return pl.pallas_call(
        functools.partial(backward_kernel, diagonal=diagonal, scaling=scaling),
        out_shape=(
            jax.ShapeDtypeStruct(dq.shape, jnp.float32),
            jax.ShapeDtypeStruct((length, HD), jnp.float32),
            jax.ShapeDtypeStruct((length, HD), jnp.float32),
        ),
        grid_spec=grid_spec,
        input_output_aliases={9: 0},
        cost_estimate=pl.CostEstimate(
            flops=10 * length * length * width,
            transcendentals=length * length * heads,
            bytes_accessed=40 * length * width,
        ),
        compiler_params=pltpu.CompilerParams(dimension_semantics=("arbitrary",)),
    )(live, query, grad, lse, rdot, key, value, qseg, kseg, dq)


def per_device(query_rows, key_rows, value_rows, out_grad, doc_lengths):
    per_kv = QH // KVH
    scaling = HD ** (-0.5)
    query_here, key_here, value_here, grad_here = (
        lax.all_to_all(query_rows, "tp", split_axis=1, concat_axis=0, tiled=True),
        lax.all_to_all(key_rows, "tp", split_axis=1, concat_axis=0, tiled=True),
        lax.all_to_all(value_rows, "tp", split_axis=1, concat_axis=0, tiled=True),
        lax.all_to_all(out_grad, "tp", split_axis=1, concat_axis=0, tiled=True),
    )
    length = query_here.shape[0]
    heads = query_here.shape[1] // HD
    seq_count = lax.axis_size("seq")
    position = lax.axis_index("seq")
    doc_ends = jnp.cumsum(doc_lengths)
    first_query = position * length
    qseg = segments(first_query, length, doc_ends).reshape(length, 1)
    first_seg = segment_of(first_query, doc_ends)
    reach = min((length - 1 + LONG - 1) // length, seq_count - 1)

    key_value = jnp.stack((key_here, value_here))
    gathered = [key_value] + [shifted(key_value, "seq", d) for d in range(1, reach + 1)]

    lives = []
    ksegs = []
    for d in range(reach + 1):
        first_key = first_query - d * length
        ksegs.append(segments(first_key, length, doc_ends).reshape(1, length))
        if d == 0:
            live = jnp.int32(1)
        else:
            last_key = first_key + length - 1
            live = ((last_key >= 0) & (segment_of(last_key, doc_ends) == first_seg)).astype(jnp.int32)
        lives.append(live.reshape(1))

    state = (
        jnp.full((heads, length, HD), -1e30, jnp.float32),
        jnp.zeros((heads, length, HD), jnp.float32),
        jnp.zeros((length, heads * HD), jnp.float32),
    )
    for d in range(reach + 1):
        state = forward_block(
            lives[d], query_here, gathered[d][0], gathered[d][1], qseg, ksegs[d], state,
            d == 0, scaling,
        )
    m, l, acc = state
    denominator = l[:, :, 0].T
    out_flat = (acc.reshape(length, heads, HD) / denominator[:, :, None]).astype(jnp.bfloat16)
    lse = m + jnp.log(l)
    rdot = jnp.sum(
        grad_here.reshape(length, heads, HD).astype(jnp.float32) * out_flat.astype(jnp.float32),
        axis=-1,
    )
    rdot = jnp.broadcast_to(rdot.T[:, :, None], (heads, length, HD))
    out_flat = out_flat.reshape(length, heads * HD)

    dq = jnp.zeros((length, heads * HD), jnp.float32)
    grad_sums = None
    for d in range(reach, -1, -1):
        dq, dk, dv = backward_block(
            lives[d], query_here, grad_here, lse, rdot, gathered[d][0], gathered[d][1],
            qseg, ksegs[d], dq, d == 0, scaling,
        )
        part = jnp.stack((dk, dv))
        if d > 0:
            part = shifted(part, "seq", -d)
        grad_sums = part if grad_sums is None else grad_sums + part

    outputs = (
        lax.all_to_all(out_flat, "tp", split_axis=0, concat_axis=1, tiled=True),
        lax.all_to_all(dq.astype(jnp.bfloat16), "tp", split_axis=0, concat_axis=1, tiled=True),
        lax.all_to_all(
            grad_sums[0].astype(jnp.bfloat16), "tp", split_axis=0, concat_axis=1, tiled=True
        ),
        lax.all_to_all(
            grad_sums[1].astype(jnp.bfloat16), "tp", split_axis=0, concat_axis=1, tiled=True
        ),
    )
    return outputs


def solution(mesh):
    return jax.shard_map(
        per_device,
        mesh=mesh,
        in_specs=(
            P(("seq", "tp"), None),
            P(("seq", "tp"), None),
            P(("seq", "tp"), None),
            P(("seq", "tp"), None),
            P(),
        ),
        out_specs=(
            P(("seq", "tp"), None),
            P(("seq", "tp"), None),
            P(("seq", "tp"), None),
            P(("seq", "tp"), None),
        ),
        check_vma=False,
    )
```

time: 299 us -> 391 us (1.31)
  Pallas kernels: 0 us -> 137 us
  matrix products: 111 us -> 0 us
  waiting for transfers between devices: 37.9 us -> 78.8 us
  starting transfers between devices: 72.4 us -> 107 us
  other arithmetic: 32 us -> 21.1 us
  local copies, waits for them, and re-layouts: 29.5 us -> 34.3 us
    pallas_call x0 -> x18, Pallas kernels: none -> 137 us  [the longest x9 74.4 us: forward_block(): pl.pallas_call(functools.partial(forward_kernel, diagonal=diagonal, scali...]
    dot_general x62 -> x0, matrix products: 111 us -> none  [the longest x9 33.8 us: absorb(): jnp.einsum('bkgt,tkd->bkgd', weight.astype(jnp.bfloat16), value_block, pr...]
    ppermute x16, starting transfers between devices: 38.1 us -> 74.3 us  [shifted(): return lax.ppermute(value, axis, pairs)]
    ppermute x16, waiting for transfers between devices: 23.3 us -> 59 us  [shifted(): return lax.ppermute(value, axis, pairs)]
    reduce_sum x11 -> x2, other arithmetic: 12.4 us -> 2.35 us  [the longest x1 1.63 us: per_device(): jnp.sum(grad_here.reshape(length, heads, HD).astype(jnp.float32) * out_fl...]
    unnamed x106 -> x49, local copies, waits for them, and re-layouts: 11.1 us -> 2.06 us
    all_to_all x1, waiting for transfers between devices: 0.01 us -> 5.93 us  [per_device(): lax.all_to_all(key_rows, 'tp', split_axis=1, concat_axis=0, tiled=True)]
    squeeze x0 -> x8, local copies, waits for them, and re-layouts: none -> 5.82 us  [per_device(): gathered[d][1]]
  transfers between devices with their start and end apart: 24 -> 24, of which waited for: 10 -> 11; matrix products, arithmetic and copies ran while one was open for 35% -> 10% of each run, Pallas kernels for 0% -> 21%
where the time goes in v2:
time: 391 us; the launch traced here: 389 us
  Pallas kernels  137 us (35%)
  starting transfers between devices  107 us (27%)
  waiting for transfers between devices  78.8 us (20%)
  local copies, waits for them, and re-layouts  34.3 us (9%)
  other arithmetic  21.1 us (5%)
  between operations  11.3 us (3%)
    pallas_call x9, Pallas kernels, forward_block(): pl.pallas_call(functools.partial(forward_kernel, diagonal=diagonal, scali...  74.4 us
    ppermute x16, starting transfers between devices, shifted(): return lax.ppermute(value, axis, pairs)  74.3 us
    pallas_call x9, Pallas kernels, backward_block(): pl.pallas_call(functools.partial(backward_kernel, diagonal=diagonal, scal...  62.7 us
    ppermute x16, waiting for transfers between devices, shifted(): return lax.ppermute(value, axis, pairs)  59 us
    another operation x8, other arithmetic, per_device(): part = jnp.stack((dk, dv))  9.8 us
  transfers between devices with their start and end apart: 24, of which 11 were waited for; matrix products, arithmetic and copies ran while one was open for 10% of the time, Pallas kernels for 21%

profile of v2, /device:TPU:16, one launch (start us, length us, event | category | flops | bytes accessed | tf_op | source)
XLA Modules:
  0.0 389.2 jit_solution(2234665479565132760)
XLA Ops:
  2.2 4.3 %all-to-all-start.2 = ((bf16[128,4,128]{2,0,1:T(8,128)(2,1)}), bf16[128,4,128]{2,0,1:T(8,128)(2,1)S(1)}, u32[]{:S(2)}, u32[]{:S(2)}) async-start(bf16[128,4,128]{2,0,1:T(8,128)(2,1)} %copy_bitcast_fusion.3), calls=%async_computation.2 | async-start | bytes 262144 | tf_op jit(solution)/shard_map/all_to_all | solution.py:185
  9.2 3.3 all-to-all-done.2
  12.5 3.3 all-to-all-start.1
  15.8 5.9 %all-to-all-done.1 = bf16[128,4,128]{2,0,1:T(8,128)(2,1)S(1)} async-done(((bf16[128,4,128]{2,0,1:T(8,128)(2,1)}), bf16[128,4,128]{2,0,1:T(8,128)(2,1)S(1)}, u32[]{:S(2)}, u32[]{:S(2)}) %all-to-all-start.1) | async-done | bytes 131104 | tf_op jit(solution)/shard_map/all_to_all | solution.py:184
  21.8 3.5 all-to-all-start
  25.3 3.2 collective-permute-start
  29.4 2.5 collective-permute-start.1
  44.9 5.3 %collective-permute-start.2 = (bf16[2,512,128]{2,1,0:T(8,128)(2,1)S(1)}, bf16[2,512,128]{2,1,0:T(8,128)(2,1)S(1)}, u32[]{:S(2)}, u32[]{:S(2)}) collective-permute-start(bf16[2,512,128]{2,1,0:T(8,128)(2,1)S(1)} %pad_maximum_fusion.8), channel_id=1, source_target_pairs={{0,24},{4,28},{8,32},{12,36},{16,40},{20,44},{24,48},{28,52},{32,5... | collective-permute-start | bytes 786440 | tf_op jit(solution)/shard_map/ppermute | solution.py:22
  56.8 2.8 collective-permute-start.6
  60.3 2.9 collective-permute-start.7
  64.6 5.0 %collective-permute-done.4 = bf16[2,512,128]{2,1,0:T(8,128)(2,1)S(1)} collective-permute-done((bf16[2,512,128]{2,1,0:T(8,128)(2,1)S(1)}, bf16[2,512,128]{2,1,0:T(8,128)(2,1)S(1)}, u32[]{:S(2)}, u32[]{:S(2)}) %collective-permute-start.4) | collective-permute-done | bytes 262176 | tf_op jit(solution)/shard_map/ppermute | solution.py:22
  70.3 3.4 collective-permute-done.5
  74.4 6.6 %collective-permute-done.6 = bf16[2,512,128]{2,1,0:T(8,128)(2,1)S(1)} collective-permute-done((bf16[2,512,128]{2,1,0:T(8,128)(2,1)S(1)}, bf16[2,512,128]{2,1,0:T(8,128)(2,1)S(1)}, u32[]{:S(2)}, u32[]{:S(2)}) %collective-permute-start.6) | collective-permute-done | bytes 262176 | tf_op jit(solution)/shard_map/ppermute | solution.py:22
  84.3 4.8 %all-to-all-start.4 = ((bf16[128,4,640]{0,2,1:T(8,128)(2,1)}), bf16[128,4,640]{0,2,1:T(8,128)(2,1)}, u32[]{:S(2)}, u32[]{:S(2)}) async-start(bf16[128,4,640]{0,2,1:T(8,128)(2,1)} %bitcast.49), calls=%async_computation.4 | async-start | bytes 1310720 | tf_op jit(solution)/shard_map/all_to_all | solution.py:186
  92.5 11.0 %shard_map.84 = (f32[5,512,128]{2,1,0:T(8,128)}, f32[5,512,128]{2,1,0:T(8,128)}, f32[512,640]{1,0:T(8,128)}) custom-call(s32[1]{0:T(128)} %constant.73.clone.1.live_ref, bf16[512,640]{1,0:T(8,128)(2,1)} %bitcast.138, bf16[512,128]{1,0:T(8,128)(2,1)} %bitcast.164, ...), custom_call_target="tpu_custom_call", output_to_operand_aliasing={{0}: (6, {}), {1}: (7, {}), {2}: (8, {})} | custom-call | flops 671088640 | bytes 13107200 | tf_op jit(solution)/shard_map/pallas_call | solution.py:121
  103.5 11.0 %shard_map.85 = (f32[5,512,128]{2,1,0:T(8,128)}, f32[5,512,128]{2,1,0:T(8,128)}, f32[512,640]{1,0:T(8,128)}) custom-call(s32[1]{0:T(128)} %bitcast.38.live_ref, bf16[512,640]{1,0:T(8,128)(2,1)} %bitcast.139, bf16[512,128]{1,0:T(8,128)(2,1)} %get-tuple-element.133.k_ref, ...), custom_call_target="tpu_custom_call", output_to_operand_aliasing={{0}: (6, {}), {1}: (7, {}), {2}: (8, {})} | custom-call | flops 671088640 | bytes 13107200 | tf_op jit(solution)/shard_map/pallas_call | solution.py:121
  114.6 11.0 %shard_map.86 = (f32[5,512,128]{2,1,0:T(8,128)}, f32[5,512,128]{2,1,0:T(8,128)}, f32[512,640]{1,0:T(8,128)}) custom-call(s32[1]{0:T(128)} %bitcast.34.live_ref, bf16[512,640]{1,0:T(8,128)(2,1)} %bitcast.140, bf16[512,128]{1,0:T(8,128)(2,1)} %get-tuple-element.135.k_ref, ...), custom_call_target="tpu_custom_call", output_to_operand_aliasing={{0}: (6, {}), {1}: (7, {}), {2}: (8, {})} | custom-call | flops 671088640 | bytes 13107200 | tf_op jit(solution)/shard_map/pallas_call | solution.py:121
  125.6 11.0 %shard_map.87 = (f32[5,512,128]{2,1,0:T(8,128)}, f32[5,512,128]{2,1,0:T(8,128)}, f32[512,640]{1,0:T(8,128)}) custom-call(s32[1]{0:T(128)} %bitcast.30.live_ref, bf16[512,640]{1,0:T(8,128)(2,1)} %bitcast.141, bf16[512,128]{1,0:T(8,128)(2,1)} %get-tuple-element.137.k_ref, ...), custom_call_target="tpu_custom_call", output_to_operand_aliasing={{0}: (6, {}), {1}: (7, {}), {2}: (8, {})} | custom-call | flops 671088640 | bytes 13107200 | tf_op jit(solution)/shard_map/pallas_call | solution.py:121
  136.6 6.1 %shard_map.88 = (f32[5,512,128]{2,1,0:T(8,128)}, f32[5,512,128]{2,1,0:T(8,128)}, f32[512,640]{1,0:T(8,128)}) custom-call(s32[1]{0:T(128)} %bitcast.26.live_ref, bf16[512,640]{1,0:T(8,128)(2,1)} %bitcast.142, bf16[512,128]{1,0:T(8,128)(2,1)} %get-tuple-element.139.k_ref, ...), custom_call_target="tpu_custom_call", output_to_operand_aliasing={{0}: (6, {}), {1}: (7, {}), {2}: (8, {})} | custom-call | flops 671088640 | bytes 13107200 | tf_op jit(solution)/shard_map/pallas_call | solution.py:121
  142.7 6.1 %shard_map.89 = (f32[5,512,128]{2,1,0:T(8,128)}, f32[5,512,128]{2,1,0:T(8,128)}, f32[512,640]{1,0:T(8,128)}) custom-call(s32[1]{0:T(128)} %bitcast.22.live_ref, bf16[512,640]{1,0:T(8,128)(2,1)} %bitcast.143, bf16[512,128]{1,0:T(8,128)(2,1)} %get-tuple-element.141.k_ref, ...), custom_call_target="tpu_custom_call", output_to_operand_aliasing={{0}: (6, {}), {1}: (7, {}), {2}: (8, {})} | custom-call | flops 671088640 | bytes 13107200 | tf_op jit(solution)/shard_map/pallas_call | solution.py:121
  148.7 6.1 %shard_map.90 = (f32[5,512,128]{2,1,0:T(8,128)}, f32[5,512,128]{2,1,0:T(8,128)}, f32[512,640]{1,0:T(8,128)}) custom-call(s32[1]{0:T(128)} %bitcast.18.live_ref, bf16[512,640]{1,0:T(8,128)(2,1)} %bitcast.144, bf16[512,128]{1,0:T(8,128)(2,1)} %get-tuple-element.143.k_ref, ...), custom_call_target="tpu_custom_call", output_to_operand_aliasing={{0}: (6, {}), {1}: (7, {}), {2}: (8, {})} | custom-call | flops 671088640 | bytes 13107200 | tf_op jit(solution)/shard_map/pallas_call | solution.py:121
  154.8 6.1 %shard_map.91 = (f32[5,512,128]{2,1,0:T(8,128)}, f32[5,512,128]{2,1,0:T(8,128)}, f32[512,640]{1,0:T(8,128)}) custom-call(s32[1]{0:T(128)} %bitcast.13.live_ref, bf16[512,640]{1,0:T(8,128)(2,1)} %bitcast.145, bf16[512,128]{1,0:T(8,128)(2,1)} %get-tuple-element.145.k_ref, ...), custom_call_target="tpu_custom_call", output_to_operand_aliasing={{0}: (6, {}), {1}: (7, {}), {2}: (8, {})} | custom-call | flops 671088640 | bytes 13107200 | tf_op jit(solution)/shard_map/pallas_call | solution.py:121
  160.8 6.1 %shard_map.92 = (f32[5,512,128]{2,1,0:T(8,128)}, f32[5,512,128]{2,1,0:T(8,128)}, f32[512,640]{1,0:T(8,128)}) custom-call(s32[1]{0:T(128)} %bitcast.2.live_ref, bf16[512,640]{1,0:T(8,128)(2,1)} %bitcast.146, bf16[512,128]{1,0:T(8,128)(2,1)} %get-tuple-element.147.k_ref, ...), custom_call_target="tpu_custom_call", output_to_operand_aliasing={{0}: (6, {}), {1}: (7, {}), {2}: (8, {})} | custom-call | flops 671088640 | bytes 13107200 | tf_op jit(solution)/shard_map/pallas_call | solution.py:121
  168.8 2.2 copy.128
  183.0 5.4 %shard_map.93 = (f32[512,640]{1,0:T(8,128)}, f32[512,128]{1,0:T(8,128)}, f32[512,128]{1,0:T(8,128)}) custom-call(s32[1]{0:T(128)} %bitcast.2.live_ref, bf16[512,640]{1,0:T(8,128)(2,1)} %bitcast.147, bf16[512,640]{1,0:T(8,128)(2,1)} %bitcast.167, f32[5,512,128]{2,1,0:T(8,128)} %log_add_fusion.lse_ref, ...), custom_call_target="tpu_custom_call", output_to_operand_aliasing={{0}: (9, {})} | custom-call | flops 1677721600 | bytes 13107200 | tf_op jit(solution)/shard_map/pallas_call | solution.py:161
  188.4 5.4 %shard_map.94 = (f32[512,640]{1,0:T(8,128)}, f32[512,128]{1,0:T(8,128)}, f32[512,128]{1,0:T(8,128)}) custom-call(s32[1]{0:T(128)} %bitcast.13.live_ref, bf16[512,640]{1,0:T(8,128)(2,1)} %bitcast.148, bf16[512,640]{1,0:T(8,128)(2,1)} %bitcast.168, f32[5,512,128]{2,1,0:T(8,128)} %log_add_fusion.lse_ref, ...), custom_call_target="tpu_custom_call", output_to_operand_aliasing={{0}: (9, {})} | custom-call | flops 1677721600 | bytes 13107200 | tf_op jit(solution)/shard_map/pallas_call | solution.py:161
  193.8 5.4 %shard_map.95 = (f32[512,640]{1,0:T(8,128)}, f32[512,128]{1,0:T(8,128)}, f32[512,128]{1,0:T(8,128)}) custom-call(s32[1]{0:T(128)} %bitcast.18.live_ref, bf16[512,640]{1,0:T(8,128)(2,1)} %bitcast.149, bf16[512,640]{1,0:T(8,128)(2,1)} %bitcast.169, f32[5,512,128]{2,1,0:T(8,128)} %log_add_fusion.lse_ref, ...), custom_call_target="tpu_custom_call", output_to_operand_aliasing={{0}: (9, {})} | custom-call | flops 1677721600 | bytes 13107200 | tf_op jit(solution)/shard_map/pallas_call | solution.py:161
  199.2 5.5 %shard_map.96 = (f32[512,640]{1,0:T(8,128)}, f32[512,128]{1,0:T(8,128)}, f32[512,128]{1,0:T(8,128)}) custom-call(s32[1]{0:T(128)} %bitcast.22.live_ref, bf16[512,640]{1,0:T(8,128)(2,1)} %bitcast.150, bf16[512,640]{1,0:T(8,128)(2,1)} %bitcast.170, f32[5,512,128]{2,1,0:T(8,128)} %log_add_fusion.lse_ref, ...), custom_call_target="tpu_custom_call", output_to_operand_aliasing={{0}: (9, {})} | custom-call | flops 1677721600 | bytes 13107200 | tf_op jit(solution)/shard_map/pallas_call | solution.py:161
  204.7 5.4 %shard_map.97 = (f32[512,640]{1,0:T(8,128)}, f32[512,128]{1,0:T(8,128)}, f32[512,128]{1,0:T(8,128)}) custom-call(s32[1]{0:T(128)} %bitcast.26.live_ref, bf16[512,640]{1,0:T(8,128)(2,1)} %bitcast.151, bf16[512,640]{1,0:T(8,128)(2,1)} %bitcast.171, f32[5,512,128]{2,1,0:T(8,128)} %log_add_fusion.lse_ref, ...), custom_call_target="tpu_custom_call", output_to_operand_aliasing={{0}: (9, {})} | custom-call | flops 1677721600 | bytes 13107200 | tf_op jit(solution)/shard_map/pallas_call | solution.py:161
  210.1 8.9 %shard_map.98 = (f32[512,640]{1,0:T(8,128)}, f32[512,128]{1,0:T(8,128)}, f32[512,128]{1,0:T(8,128)}) custom-call(s32[1]{0:T(128)} %bitcast.30.live_ref, bf16[512,640]{1,0:T(8,128)(2,1)} %bitcast.152, bf16[512,640]{1,0:T(8,128)(2,1)} %bitcast.172, f32[5,512,128]{2,1,0:T(8,128)} %log_add_fusion.lse_ref, ...), custom_call_target="tpu_custom_call", output_to_operand_aliasing={{0}: (9, {})} | custom-call | flops 1677721600 | bytes 13107200 | tf_op jit(solution)/shard_map/pallas_call | solution.py:161
  219.0 9.2 %shard_map.99 = (f32[512,640]{1,0:T(8,128)}, f32[512,128]{1,0:T(8,128)}, f32[512,128]{1,0:T(8,128)}) custom-call(s32[1]{0:T(128)} %bitcast.34.live_ref, bf16[512,640]{1,0:T(8,128)(2,1)} %bitcast.153, bf16[512,640]{1,0:T(8,128)(2,1)} %bitcast.173, f32[5,512,128]{2,1,0:T(8,128)} %log_add_fusion.lse_ref, ...), custom_call_target="tpu_custom_call", output_to_operand_aliasing={{0}: (9, {})} | custom-call | flops 1677721600 | bytes 13107200 | tf_op jit(solution)/shard_map/pallas_call | solution.py:161
  228.2 9.0 %shard_map.100 = (f32[512,640]{1,0:T(8,128)}, f32[512,128]{1,0:T(8,128)}, f32[512,128]{1,0:T(8,128)}) custom-call(s32[1]{0:T(128)} %bitcast.38.live_ref, bf16[512,640]{1,0:T(8,128)(2,1)} %bitcast.154, bf16[512,640]{1,0:T(8,128)(2,1)} %bitcast.174, f32[5,512,128]{2,1,0:T(8,128)} %log_add_fusion.lse_ref, ...), custom_call_target="tpu_custom_call", output_to_operand_aliasing={{0}: (9, {})} | custom-call | flops 1677721600 | bytes 13107200 | tf_op jit(solution)/shard_map/pallas_call | solution.py:161
  244.8 14.8 %collective-permute-start.13 = (f32[2,512,128]{2,1,0:T(8,128)}, f32[2,512,128]{2,1,0:T(8,128)}, u32[]{:S(2)}, u32[]{:S(2)}) collective-permute-start(f32[2,512,128]{2,1,0:T(8,128)} %pad_maximum_fusion.5), channel_id=1, source_target_pairs={{12,0},{16,4},{20,8},{24,12},{28,16},{32,20},{36,24},{40,28},{44,3... | collective-permute-start | bytes 1572872 | tf_op jit(solution)/shard_map/ppermute | solution.py:22
  263.4 15.7 %collective-permute-start.12 = (f32[2,512,128]{2,1,0:T(8,128)}, f32[2,512,128]{2,1,0:T(8,128)}, u32[]{:S(2)}, u32[]{:S(2)}) collective-permute-start(f32[2,512,128]{2,1,0:T(8,128)} %pad_maximum_fusion.4), channel_id=1, source_target_pairs={{16,0},{20,4},{24,8},{28,12},{32,16},{36,20},{40,24},{44,28},{48,3... | collective-permute-start | bytes 1572872 | tf_op jit(solution)/shard_map/ppermute | solution.py:22
  281.1 2.0 collective-permute-start.11
  288.6 2.1 collective-permute-start.8
  290.7 11.4 %collective-permute-start.9 = (f32[2,512,128]{2,1,0:T(8,128)}, f32[2,512,128]{2,1,0:T(8,128)}, u32[]{:S(2)}, u32[]{:S(2)}) collective-permute-start(f32[2,512,128]{2,1,0:T(8,128)} %pad_maximum_fusion.1), channel_id=1, source_target_pairs={{28,0},{32,4},{36,8},{40,12},{44,16},{48,20},{52,24},{56,28},{60,3... | collective-permute-start | bytes 1572872 | tf_op jit(solution)/shard_map/ppermute | solution.py:22
  303.1 4.8 %all-to-all-start.3 = ((bf16[4,128,640]{2,1,0:T(8,128)(2,1)}), bf16[4,128,640]{2,1,0:T(8,128)(2,1)S(1)}, u32[]{:S(2)}, u32[]{:S(2)}) async-start(bf16[4,128,640]{2,1,0:T(8,128)(2,1)} %bitcast.47), calls=%async_computation.3 | async-start | bytes 1310720 | tf_op jit(solution)/shard_map/all_to_all | solution.py:247
  307.9 8.5 %shard_map.101 = (f32[512,640]{1,0:T(8,128)}, f32[512,128]{1,0:T(8,128)}, f32[512,128]{1,0:T(8,128)}) custom-call(s32[1]{0:T(128)} %constant.73.clone.1.live_ref, bf16[512,640]{1,0:T(8,128)(2,1)} %bitcast.155, bf16[512,640]{1,0:T(8,128)(2,1)} %bitcast.175, f32[5,512,128]{2,1,0:T(8,128)} %log_add_fusion.lse_ref, ...), custom_call_target="tpu_custom_call", output_to_operand_aliasing={{0}: (9, {})} | custom-call | flops 1677721600 | bytes 13107200 | tf_op jit(solution)/shard_map/pallas_call | solution.py:161
  316.4 2.3 convert_element_type.114
  319.8 3.7 all-to-all-start.5
  323.5 3.1 collective-permute-done.10
  326.6 39.0 %collective-permute-done.8 = f32[2,512,128]{2,1,0:T(8,128)} collective-permute-done((f32[2,512,128]{2,1,0:T(8,128)}, f32[2,512,128]{2,1,0:T(8,128)}, u32[]{:S(2)}, u32[]{:S(2)}) %collective-permute-start.8) | collective-permute-done | bytes 524320 | tf_op jit(solution)/shard_map/ppermute | solution.py:22
  365.7 2.2 fusion
  368.6 4.7 %all-to-all-start.6 = ((bf16[4,128,128]{2,1,0:T(8,128)(2,1)}), bf16[4,128,128]{2,1,0:T(8,128)(2,1)S(1)}, u32[]{:S(2)}, u32[]{:S(2)}) async-start(bf16[4,128,128]{2,1,0:T(8,128)(2,1)} %bitcast.76), calls=%async_computation.6 | async-start | bytes 262144 | tf_op jit(solution)/shard_map/all_to_all | solution.py:249
  375.0 4.2 %all-to-all-done.6 = bf16[4,128,128]{2,1,0:T(8,128)(2,1)S(1)} async-done(((bf16[4,128,128]{2,1,0:T(8,128)(2,1)}), bf16[4,128,128]{2,1,0:T(8,128)(2,1)S(1)}, u32[]{:S(2)}, u32[]{:S(2)}) %all-to-all-start.6) | async-done | bytes 131104 | tf_op jit(solution)/shard_map/all_to_all | solution.py:249
  379.2 3.3 all-to-all-start.7
  383.2 5.3 %all-to-all-done.7 = bf16[4,128,128]{2,1,0:T(8,128)(2,1)S(1)} async-done(((bf16[4,128,128]{2,1,0:T(8,128)(2,1)}), bf16[4,128,128]{2,1,0:T(8,128)(2,1)S(1)}, u32[]{:S(2)}, u32[]{:S(2)}) %all-to-all-start.7) | async-done | bytes 131104 | tf_op jit(solution)/shard_map/all_to_all | solution.py:252
  (119 shorter events, 63.3 us)
Async XLA Ops:
  0.6 0.9 copy-start
  0.6 7.8 %copy-start.21 = (bf16[128,512]{1,0:T(8,128)(2,1)S(1)}, bf16[128,512]{1,0:T(8,128)(2,1)}, u32[]{:S(2)}) copy-start(bf16[128,512]{1,0:T(8,128)(2,1)} %param.6) | copy-start | bytes 393220
  2.2 10.3 %all-to-all-start.2 = ((bf16[128,4,128]{2,0,1:T(8,128)(2,1)}), bf16[128,4,128]{2,0,1:T(8,128)(2,1)S(1)}, u32[]{:S(2)}, u32[]{:S(2)}) async-start(bf16[128,4,128]{2,0,1:T(8,128)(2,1)} %copy_bitcast_fusion.3), calls=%async_computation.2 | async-start | bytes 262144 | tf_op jit(solution)/shard_map/all_to_all | solution.py:185
  8.5 20.0 %copy-start.23 = (s32[8]{0:T(128)S(1)}, s32[8]{0:T(128)}, u32[]{:S(2)}) copy-start(s32[8]{0:T(128)} %param.9) | copy-start | bytes 100
  9.2 34.6 %copy-start.7 = (bf16[128,2560]{1,0:T(8,128)(2,1)S(1)}, bf16[128,2560]{1,0:T(8,128)(2,1)}, u32[]{:S(2)}) copy-start(bf16[128,2560]{1,0:T(8,128)(2,1)} %param.8) | copy-start | bytes 1966084
  12.5 32.4 %copy-start.5 = (bf16[128,4,128]{2,0,1:T(8,128)(2,1)}, bf16[128,4,128]{2,0,1:T(8,128)(2,1)S(1)}, u32[]{:S(2)}) copy-start(bf16[128,4,128]{2,0,1:T(8,128)(2,1)S(1)} %all-to-all-done.2) | copy-start | bytes 393220
  12.5 9.3 %all-to-all-start.1 = ((bf16[128,4,128]{2,0,1:T(8,128)(2,1)}), bf16[128,4,128]{2,0,1:T(8,128)(2,1)S(1)}, u32[]{:S(2)}, u32[]{:S(2)}) async-start(bf16[128,4,128]{2,0,1:T(8,128)(2,1)} %copy_bitcast_fusion.4), calls=%async_computation.1 | async-start | bytes 262144 | tf_op jit(solution)/shard_map/all_to_all | solution.py:184
  21.8 23.1 %copy-start.6 = (bf16[128,4,128]{2,0,1:T(8,128)(2,1)}, bf16[128,4,128]{2,0,1:T(8,128)(2,1)S(1)}, u32[]{:S(2)}) copy-start(bf16[128,4,128]{2,0,1:T(8,128)(2,1)S(1)} %all-to-all-done.1) | copy-start | bytes 393220
  21.8 62.5 %all-to-all-start = ((bf16[128,4,640]{2,0,1:T(8,128)(2,1)}), bf16[128,4,640]{2,0,1:T(8,128)(2,1)S(1)}, u32[]{:S(2)}, u32[]{:S(2)}) async-start(bf16[128,4,640]{2,0,1:T(8,128)(2,1)} %bitcast.137), calls=%async_computation | async-start | bytes 1310720 | tf_op jit(solution)/shard_map/all_to_all | solution.py:183
  25.3 28.8 %collective-permute-start = (bf16[2,512,128]{2,1,0:T(8,128)(2,1)S(1)}, bf16[2,512,128]{2,1,0:T(8,128)(2,1)S(1)}, u32[]{:S(2)}, u32[]{:S(2)}) collective-permute-start(bf16[2,512,128]{2,1,0:T(8,128)(2,1)S(1)} %pad_maximum_fusion.8), channel_id=1, source_target_pairs={{0,32},{4,36},{8,40},{12,44},{16,48},{20,52},{24,56},{28,60},{32,6... | collective-permute-start | bytes 786440 | tf_op jit(solution)/shard_map/ppermute | solution.py:22
  29.4 30.8 %copy-start.22 = (s32[512]{0:T(512)}, s32[512]{0:T(512)S(1)}, u32[]{:S(2)}) copy-start(s32[512]{0:T(512)S(1)} %get-tuple-element.119) | copy-start | bytes 6148
  29.4 27.4 %collective-permute-start.1 = (bf16[2,512,128]{2,1,0:T(8,128)(2,1)S(1)}, bf16[2,512,128]{2,1,0:T(8,128)(2,1)S(1)}, u32[]{:S(2)}, u32[]{:S(2)}) collective-permute-start(bf16[2,512,128]{2,1,0:T(8,128)(2,1)S(1)} %pad_maximum_fusion.8), channel_id=1, source_target_pairs={{0,28},{4,32},{8,36},{12,40},{16,44},{20,48},{24,52},{28,56},{32,6... | collective-permute-start | bytes 786440 | tf_op jit(solution)/shard_map/ppermute | solution.py:22
  44.9 15.3 %collective-permute-start.2 = (bf16[2,512,128]{2,1,0:T(8,128)(2,1)S(1)}, bf16[2,512,128]{2,1,0:T(8,128)(2,1)S(1)}, u32[]{:S(2)}, u32[]{:S(2)}) collective-permute-start(bf16[2,512,128]{2,1,0:T(8,128)(2,1)S(1)} %pad_maximum_fusion.8), channel_id=1, source_target_pairs={{0,24},{4,28},{8,32},{12,36},{16,40},{20,44},{24,48},{28,52},{32,5... | collective-permute-start | bytes 786440 | tf_op jit(solution)/shard_map/ppermute | solution.py:22
  50.3 13.6 %collective-permute-start.3 = (bf16[2,512,128]{2,1,0:T(8,128)(2,1)S(1)}, bf16[2,512,128]{2,1,0:T(8,128)(2,1)S(1)}, u32[]{:S(2)}, u32[]{:S(2)}) collective-permute-start(bf16[2,512,128]{2,1,0:T(8,128)(2,1)S(1)} %pad_maximum_fusion.8), channel_id=1, source_target_pairs={{0,20},{4,24},{8,28},{12,32},{16,36},{20,40},{24,44},{28,48},{32,5... | collective-permute-start | bytes 786440 | tf_op jit(solution)/shard_map/ppermute | solution.py:22
  52.2 17.4 %collective-permute-start.4 = (bf16[2,512,128]{2,1,0:T(8,128)(2,1)S(1)}, bf16[2,512,128]{2,1,0:T(8,128)(2,1)S(1)}, u32[]{:S(2)}, u32[]{:S(2)}) collective-permute-start(bf16[2,512,128]{2,1,0:T(8,128)(2,1)S(1)} %pad_maximum_fusion.8), channel_id=1, source_target_pairs={{0,16},{4,20},{8,24},{12,28},{16,32},{20,36},{24,40},{28,44},{32,4... | collective-permute-start | bytes 786440 | tf_op jit(solution)/shard_map/ppermute | solution.py:22
  54.1 19.6 %collective-permute-start.5 = (bf16[2,512,128]{2,1,0:T(8,128)(2,1)S(1)}, bf16[2,512,128]{2,1,0:T(8,128)(2,1)S(1)}, u32[]{:S(2)}, u32[]{:S(2)}) collective-permute-start(bf16[2,512,128]{2,1,0:T(8,128)(2,1)S(1)} %pad_maximum_fusion.8), channel_id=1, source_target_pairs={{0,12},{4,16},{8,20},{12,24},{16,28},{20,32},{24,36},{28,40},{32,4... | collective-permute-start | bytes 786440 | tf_op jit(solution)/shard_map/ppermute | solution.py:22
  56.8 24.3 %collective-permute-start.6 = (bf16[2,512,128]{2,1,0:T(8,128)(2,1)S(1)}, bf16[2,512,128]{2,1,0:T(8,128)(2,1)S(1)}, u32[]{:S(2)}, u32[]{:S(2)}) collective-permute-start(bf16[2,512,128]{2,1,0:T(8,128)(2,1)S(1)} %pad_maximum_fusion.8), channel_id=1, source_target_pairs={{0,8},{4,12},{8,16},{12,20},{16,24},{20,28},{24,32},{28,36},{32,40... | collective-permute-start | bytes 786440 | tf_op jit(solution)/shard_map/ppermute | solution.py:22
  60.3 23.3 %collective-permute-start.7 = (bf16[2,512,128]{2,1,0:T(8,128)(2,1)S(1)}, bf16[2,512,128]{2,1,0:T(8,128)(2,1)S(1)}, u32[]{:S(2)}, u32[]{:S(2)}) collective-permute-start(bf16[2,512,128]{2,1,0:T(8,128)(2,1)S(1)} %pad_maximum_fusion.8), channel_id=1, source_target_pairs={{0,4},{4,8},{8,12},{12,16},{16,20},{20,24},{24,28},{28,32},{32,36}... | collective-permute-start | bytes 786440 | tf_op jit(solution)/shard_map/ppermute | solution.py:22
  84.3 5.9 %copy-start.4 = (bf16[128,4,640]{2,0,1:T(8,128)(2,1)}, bf16[128,4,640]{2,0,1:T(8,128)(2,1)S(1)}, u32[]{:S(2)}) copy-start(bf16[128,4,640]{2,0,1:T(8,128)(2,1)S(1)} %all-to-all-done) | copy-start | bytes 1966084
  84.3 84.5 %all-to-all-start.4 = ((bf16[128,4,640]{0,2,1:T(8,128)(2,1)}), bf16[128,4,640]{0,2,1:T(8,128)(2,1)}, u32[]{:S(2)}, u32[]{:S(2)}) async-start(bf16[128,4,640]{0,2,1:T(8,128)(2,1)} %bitcast.49), calls=%async_computation.4 | async-start | bytes 1310720 | tf_op jit(solution)/shard_map/all_to_all | solution.py:186
  166.9 4.1 %copy-start.1 = (f32[5,512,128]{2,1,0:T(8,128)S(1)}, f32[5,512,128]{2,1,0:T(8,128)}, u32[]{:S(2)}) copy-start(f32[5,512,128]{2,1,0:T(8,128)} %get-tuple-element.83) | copy-start | bytes 3932164
  166.9 4.1 %copy-start.3 = (f32[5,512,128]{2,1,0:T(8,128)S(1)}, f32[5,512,128]{2,1,0:T(8,128)}, u32[]{:S(2)}) copy-start(f32[5,512,128]{2,1,0:T(8,128)} %get-tuple-element.84) | copy-start | bytes 3932164
  175.3 1.9 copy-start.2
  228.2 13.0 %copy-start.19 = (f32[512,128]{1,0:T(8,128)S(1)}, f32[512,128]{1,0:T(8,128)}, u32[]{:S(2)}) copy-start(f32[512,128]{1,0:T(8,128)} %get-tuple-element.106) | copy-start | bytes 786436
  228.2 13.0 %copy-start.20 = (f32[512,128]{1,0:T(8,128)S(1)}, f32[512,128]{1,0:T(8,128)}, u32[]{:S(2)}) copy-start(f32[512,128]{1,0:T(8,128)} %get-tuple-element.107) | copy-start | bytes 786436
  237.2 6.8 %copy-start.17 = (f32[512,128]{1,0:T(8,128)S(1)}, f32[512,128]{1,0:T(8,128)}, u32[]{:S(2)}) copy-start(f32[512,128]{1,0:T(8,128)} %get-tuple-element.104) | copy-start | bytes 786436
  237.2 6.8 %copy-start.18 = (f32[512,128]{1,0:T(8,128)S(1)}, f32[512,128]{1,0:T(8,128)}, u32[]{:S(2)}) copy-start(f32[512,128]{1,0:T(8,128)} %get-tuple-element.105) | copy-start | bytes 786436
  239.1 20.4 %copy-start.15 = (f32[512,128]{1,0:T(8,128)S(1)}, f32[512,128]{1,0:T(8,128)}, u32[]{:S(2)}) copy-start(f32[512,128]{1,0:T(8,128)} %get-tuple-element.102) | copy-start | bytes 786436
  239.1 20.4 %copy-start.16 = (f32[512,128]{1,0:T(8,128)S(1)}, f32[512,128]{1,0:T(8,128)}, u32[]{:S(2)}) copy-start(f32[512,128]{1,0:T(8,128)} %get-tuple-element.103) | copy-start | bytes 786436
  239.1 47.5 %collective-permute-start.15 = (f32[2,512,128]{2,1,0:T(8,128)}, f32[2,512,128]{2,1,0:T(8,128)S(1)}, u32[]{:S(2)}, u32[]{:S(2)}) collective-permute-start(f32[2,512,128]{2,1,0:T(8,128)} %pad_maximum_fusion.7), channel_id=1, source_target_pairs={{4,0},{8,4},{12,8},{16,12},{20,16},{24,20},{28,24},{32,28},{36,32}... | collective-permute-start | bytes 1572872 | tf_op jit(solution)/shard_map/ppermute | solution.py:22
  242.0 46.5 %collective-permute-start.14 = (f32[2,512,128]{2,1,0:T(8,128)}, f32[2,512,128]{2,1,0:T(8,128)}, u32[]{:S(2)}, u32[]{:S(2)}) collective-permute-start(f32[2,512,128]{2,1,0:T(8,128)} %pad_maximum_fusion.6), channel_id=1, source_target_pairs={{8,0},{12,4},{16,8},{20,12},{24,16},{28,20},{32,24},{36,28},{40,32... | collective-permute-start | bytes 1572872 | tf_op jit(solution)/shard_map/ppermute | solution.py:22
  244.8 45.9 %collective-permute-start.13 = (f32[2,512,128]{2,1,0:T(8,128)}, f32[2,512,128]{2,1,0:T(8,128)}, u32[]{:S(2)}, u32[]{:S(2)}) collective-permute-start(f32[2,512,128]{2,1,0:T(8,128)} %pad_maximum_fusion.5), channel_id=1, source_target_pairs={{12,0},{16,4},{20,8},{24,12},{28,16},{32,20},{36,24},{40,28},{44,3... | collective-permute-start | bytes 1572872 | tf_op jit(solution)/shard_map/ppermute | solution.py:22
  261.6 21.5 %copy-start.14 = (f32[512,128]{1,0:T(8,128)S(1)}, f32[512,128]{1,0:T(8,128)}, u32[]{:S(2)}) copy-start(f32[512,128]{1,0:T(8,128)} %get-tuple-element.98) | copy-start | bytes 786436
  263.4 21.5 %copy-start.10 = (f32[512,128]{1,0:T(8,128)S(1)}, f32[512,128]{1,0:T(8,128)}, u32[]{:S(2)}) copy-start(f32[512,128]{1,0:T(8,128)} %get-tuple-element.94) | copy-start | bytes 786436
  263.4 21.5 %copy-start.11 = (f32[512,128]{1,0:T(8,128)S(1)}, f32[512,128]{1,0:T(8,128)}, u32[]{:S(2)}) copy-start(f32[512,128]{1,0:T(8,128)} %get-tuple-element.95) | copy-start | bytes 786436
  263.4 60.0 %collective-permute-start.12 = (f32[2,512,128]{2,1,0:T(8,128)}, f32[2,512,128]{2,1,0:T(8,128)}, u32[]{:S(2)}, u32[]{:S(2)}) collective-permute-start(f32[2,512,128]{2,1,0:T(8,128)} %pad_maximum_fusion.4), channel_id=1, source_target_pairs={{16,0},{20,4},{24,8},{28,12},{32,16},{36,20},{40,24},{44,28},{48,3... | collective-permute-start | bytes 1572872 | tf_op jit(solution)/shard_map/ppermute | solution.py:22
  281.1 4.8 %copy-start.12 = (f32[512,128]{1,0:T(8,128)S(1)}, f32[512,128]{1,0:T(8,128)}, u32[]{:S(2)}) copy-start(f32[512,128]{1,0:T(8,128)} %get-tuple-element.96) | copy-start | bytes 786436
  281.1 4.8 %copy-start.13 = (f32[512,128]{1,0:T(8,128)S(1)}, f32[512,128]{1,0:T(8,128)}, u32[]{:S(2)}) copy-start(f32[512,128]{1,0:T(8,128)} %get-tuple-element.97) | copy-start | bytes 786436
  281.1 42.4 %collective-permute-start.11 = (f32[2,512,128]{2,1,0:T(8,128)}, f32[2,512,128]{2,1,0:T(8,128)}, u32[]{:S(2)}, u32[]{:S(2)}) collective-permute-start(f32[2,512,128]{2,1,0:T(8,128)} %pad_maximum_fusion.3), channel_id=1, source_target_pairs={{20,0},{24,4},{28,8},{32,12},{36,16},{40,20},{44,24},{48,28},{52,3... | collective-permute-start | bytes 1572872 | tf_op jit(solution)/shard_map/ppermute | solution.py:22
  286.7 40.0 %collective-permute-start.10 = (f32[2,512,128]{2,1,0:T(8,128)}, f32[2,512,128]{2,1,0:T(8,128)}, u32[]{:S(2)}, u32[]{:S(2)}) collective-permute-start(f32[2,512,128]{2,1,0:T(8,128)} %pad_maximum_fusion.2), channel_id=1, source_target_pairs={{24,0},{28,4},{32,8},{36,12},{40,16},{44,20},{48,24},{52,28},{56,3... | collective-permute-start | bytes 1572872 | tf_op jit(solution)/shard_map/ppermute | solution.py:22
  288.6 77.1 %collective-permute-start.8 = (f32[2,512,128]{2,1,0:T(8,128)}, f32[2,512,128]{2,1,0:T(8,128)}, u32[]{:S(2)}, u32[]{:S(2)}) collective-permute-start(f32[2,512,128]{2,1,0:T(8,128)} %pad_maximum_fusion), channel_id=1, source_target_pairs={{32,0},{36,4},{40,8},{44,12},{48,16},{52,20},{56,24},{60,28},{64,3... | collective-permute-start | bytes 1572872 | tf_op jit(solution)/shard_map/ppermute | solution.py:22
  290.7 75.0 %collective-permute-start.9 = (f32[2,512,128]{2,1,0:T(8,128)}, f32[2,512,128]{2,1,0:T(8,128)}, u32[]{:S(2)}, u32[]{:S(2)}) collective-permute-start(f32[2,512,128]{2,1,0:T(8,128)} %pad_maximum_fusion.1), channel_id=1, source_target_pairs={{28,0},{32,4},{36,8},{40,12},{44,16},{48,20},{52,24},{56,28},{60,3... | collective-permute-start | bytes 1572872 | tf_op jit(solution)/shard_map/ppermute | solution.py:22
  303.1 16.7 %all-to-all-start.3 = ((bf16[4,128,640]{2,1,0:T(8,128)(2,1)}), bf16[4,128,640]{2,1,0:T(8,128)(2,1)S(1)}, u32[]{:S(2)}, u32[]{:S(2)}) async-start(bf16[4,128,640]{2,1,0:T(8,128)(2,1)} %bitcast.47), calls=%async_computation.3 | async-start | bytes 1310720 | tf_op jit(solution)/shard_map/all_to_all | solution.py:247
  316.4 49.3 %copy-start.8 = (f32[512,128]{1,0:T(8,128)S(1)}, f32[512,128]{1,0:T(8,128)}, u32[]{:S(2)}) copy-start(f32[512,128]{1,0:T(8,128)} %get-tuple-element.110) | copy-start | bytes 786436
  316.4 49.3 %copy-start.9 = (f32[512,128]{1,0:T(8,128)S(1)}, f32[512,128]{1,0:T(8,128)}, u32[]{:S(2)}) copy-start(f32[512,128]{1,0:T(8,128)} %get-tuple-element.111) | copy-start | bytes 786436
  319.8 48.8 %all-to-all-start.5 = ((bf16[4,128,640]{2,1,0:T(8,128)(2,1)}), bf16[4,128,640]{2,1,0:T(8,128)(2,1)S(1)}, u32[]{:S(2)}, u32[]{:S(2)}) async-start(bf16[4,128,640]{2,1,0:T(8,128)(2,1)} %bitcast.56), calls=%async_computation.5 | async-start | bytes 1310720 | tf_op jit(solution)/shard_map/all_to_all | solution.py:248
  368.6 10.6 %all-to-all-start.6 = ((bf16[4,128,128]{2,1,0:T(8,128)(2,1)}), bf16[4,128,128]{2,1,0:T(8,128)(2,1)S(1)}, u32[]{:S(2)}, u32[]{:S(2)}) async-start(bf16[4,128,128]{2,1,0:T(8,128)(2,1)} %bitcast.76), calls=%async_computation.6 | async-start | bytes 262144 | tf_op jit(solution)/shard_map/all_to_all | solution.py:249
  379.2 9.3 %all-to-all-start.7 = ((bf16[4,128,128]{2,1,0:T(8,128)(2,1)}), bf16[4,128,128]{2,1,0:T(8,128)(2,1)S(1)}, u32[]{:S(2)}, u32[]{:S(2)}) async-start(bf16[4,128,128]{2,1,0:T(8,128)(2,1)} %bitcast.78), calls=%async_computation.7 | async-start | bytes 262144 | tf_op jit(solution)/shard_map/all_to_all | solution.py:252
